TPU v7x, 32 devices: a whole 2x2x4 slice. The times are simulated.
32 devices in a mesh: occ: 4 (over z), vir: 8 (over y, x, core).
Axes of the slice: x: 2, y: 2, z: 4, core: 2. Of those that a mesh axis runs over, the one named last changes fastest.
Arguments:
- lam: bfloat16 [4096, 12288], P('occ', 'vir'), may hold values from -6 to 6
- integrals: bfloat16 [12288, 1024], P('vir', 'occ'), may hold values from -0.21875 to 0.21875
- occ_sym: int32 [32], P('occ'), may hold values from 0 to 7, as said below
- cd_sym: int32 [96], P('vir'), may hold values from 0 to 7
- ab_sym: int32 [8], replicated, may hold values from 0 to 7
Outputs:
- ladder: bfloat16 [4096, 1024], P('occ', 'vir')
Inputs may be any that keep to these rules, and one draw needn't show every extreme that they name: `occ_sym`: in each aligned block of 8 tiles (those of one index of occ) each representation labels the same number of tiles, 1 of them.
All inputs are finite; a program needn't handle non-finite values.
Results may differ from a plain program's by a relative error of at most 0.001.
Values may be sent and summed in bfloat16 or wider, within the bound.
No kernel may reach another device: no remote copies, remote signals or barrier semaphores. Data moves between devices by JAX's collectives and lax.ppermute only.
A program may use at most 128 MiB of HBM per device.

v0:
```python
import jax
import jax.numpy as jnp
from jax import lax
from jax.sharding import PartitionSpec as P


def halving_reduce_scatter(parts, axis):
    n = lax.axis_size(axis)
    me = lax.axis_index(axis)
    step = 1
    while step < n:
        bit = (me // step) % 2
        pairs = parts.reshape(parts.shape[0] // 2, 2, *parts.shape[1:])
        keep = lax.dynamic_index_in_dim(pairs, bit, axis=1, keepdims=False)
        send = lax.dynamic_index_in_dim(pairs, 1 - bit, axis=1, keepdims=False)
        perm = [(j, j ^ step) for j in range(n)]
        parts = keep + lax.ppermute(send, axis, perm)
        step *= 2
    return parts[0]


def doubling_max(value, axis):
    n = lax.axis_size(axis)
    step = 1
    while step < n:
        value = jnp.maximum(value, lax.ppermute(value, axis, [(j, j ^ step) for j in range(n)]))
        step *= 2
    return value


def line_gather(x, axis):
    n = lax.axis_size(axis)
    me = lax.axis_index(axis)
    rightward = [(a, a + 1) for a in range(n - 1)]
    leftward = [(a, a - 1) for a in range(1, n)]
    lefts, rights = [], []
    from_left, from_right = x, x
    for _ in range(1, n):
        from_left = lax.ppermute(from_left, axis, rightward)
        from_right = lax.ppermute(from_right, axis, leftward)
        lefts.append(from_left)
        rights.append(from_right)
    line = jnp.concatenate(lefts[::-1] + [x] + rights)
    return lax.dynamic_slice_in_dim(line, (n - 1 - me) * x.shape[0], n * x.shape[0])


def packed_partials(lam_kept, int_kept, order, valid, col_of, col_tiles, cap):
    received = line_gather(int_kept[:cap], "occ")
    q = order[:, :cap].reshape(-1)
    t = col_of[:, :cap].reshape(-1)
    ok = valid[:, :cap].reshape(-1)
    lam_tiles = jnp.where(ok[:, None, None], lam_kept[q], jnp.zeros((), lam_kept.dtype))
    products = jnp.einsum(
        "srm,smc->src", lam_tiles, received, preferred_element_type=jnp.float32
    )
    onehot = (t[None, :] == jnp.arange(col_tiles)[:, None]) & ok[None, :]
    return jnp.einsum(
        "ts,src->trc", onehot.astype(jnp.float32), products, precision=lax.Precision.HIGHEST
    )


def on_device(lam, integrals, occ_sym, cd_sym, ab_sym):
    row_tiles = occ_sym.shape[0]
    cd_tiles = cd_sym.shape[0]
    tile_edge = lam.shape[0] // row_tiles
    col_tiles = ab_sym.shape[0]
    own_cols = integrals.shape[1] // tile_edge
    peers = col_tiles // own_cols
    row_of = jnp.argmax(occ_sym[None, :] == ab_sym[:, None], axis=1)
    kept = cd_sym[:, None] == ab_sym[None, :]
    kept = kept.reshape(cd_tiles, peers, own_cols).transpose(1, 0, 2)
    need = jnp.max(jnp.sum(kept, axis=(1, 2)))
    dense = cd_tiles * own_cols
    flat = kept.reshape(peers, dense)
    rank = jnp.cumsum(flat, axis=1) - 1
    hit = flat[:, None, :] & (rank[:, None, :] == jnp.arange(dense)[None, :, None])
    slot = jnp.sum(hit * jnp.arange(dense), axis=2)
    valid = jnp.any(hit, axis=2)
    order = slot // own_cols
    col_of = jnp.arange(peers)[:, None] * own_cols + slot % own_cols
    me = lax.axis_index("occ")
    blocks = integrals.reshape(cd_tiles, tile_edge, own_cols * tile_edge)[order[me]]
    int_kept = blocks[:, :, :tile_edge]
    for col in range(1, own_cols):
        pick = (slot[me] % own_cols == col)[:, None, None]
        int_kept = jnp.where(pick, blocks[:, :, col * tile_edge:(col + 1) * tile_edge], int_kept)
    row_for_q = jnp.argmax(occ_sym[:, None] == cd_sym[None, :], axis=0)
    lam3 = lam.reshape(row_tiles, tile_edge, cd_tiles * tile_edge)
    pick = jnp.repeat(row_for_q[None, :] == jnp.arange(row_tiles)[:, None], tile_edge, axis=1)
    lam_kept = jnp.sum(jnp.where(pick[:, None, :], lam3, jnp.zeros((), lam.dtype)), axis=0)
    lam_kept = lam_kept.reshape(tile_edge, cd_tiles, tile_edge).transpose(1, 0, 2)
    caps = sorted({max(1, dense // 3), max(1, dense // 2), dense})
    branch = sum((need > cap).astype(jnp.int32) for cap in caps[:-1])
    partial_sum = lax.switch(
        branch,
        [
            lambda l, i, cap=cap: packed_partials(l, i, order, valid, col_of, col_tiles, cap)
            for cap in caps
        ],
        lam_kept,
        int_kept,
    )
    summed = halving_reduce_scatter(partial_sum, "vir")
    own_row = row_of[lax.axis_index("vir")]
    keep = (jnp.arange(row_tiles) == own_row)[:, None, None]
    out = jnp.where(keep, summed.astype(jnp.bfloat16)[None], jnp.zeros((), jnp.bfloat16))
    return out.reshape(row_tiles * tile_edge, summed.shape[1])


def solution(mesh):
    in_specs = (P("occ", "vir"), P("vir", "occ"), P("occ"), P("vir"), P())
    out_specs = P("occ", "vir")
    return jax.shard_map(
        on_device, mesh=mesh, in_specs=in_specs, out_specs=out_specs, check_vma=False
    )
```

profile of v0, /device:TPU:0, one launch (start us, length us, event | category | flops | bytes accessed | tf_op | source)
XLA Modules:
  0.0 61.2 jit_solution(9514499365740518307)
XLA Ops:
  5.6 1.3 %iota_reduce_fusion = (pred[12]{0:T(512)(128)(4,1)}, s32[12]{0:T(128)S(1)}) fusion(s32[12]{0:T(128)} %param.11, s32[8]{0:T(128)} %param.10), kind=kLoop, calls=%fused_computation.92 | loop fusion | flops 684 | bytes 140 | tf_op jit(solution)/shard_map/on_device/reduce | solution.py:87
  7.0 2.7 %select_reduce_fusion = bf16[128,1536]{1,0:T(8,128)(2,1)S(1)} fusion(bf16[8,128,1536]{2,1,0:T(8,128)(2,1)} %bitcast.65, pred[8,1536]{1,0:T(8,128)(4,1)S(1)} %broadcast_bitcast_fusion), kind=kLoop, calls=%fused_computation.76 | loop fusion | flops 2949120 | bytes 3551232 | tf_op jit(solution)/shard_map/reduce_sum | solution.py:90
  10.9 37.0 %conditional.1 = (f32[4,2,128,128]{3,1,0,2:T(2,128)S(1)}) conditional(s32[]{:T(128)} %clamp.3, (s32[4,24]{1,0:T(4,128)S(1)}, pred[4,24]{1,0:T(4,128)(4,1)}, s32[4,24]{1,0:T(4,128)S(1)}, bf16[12,128,128]{1,2,0:T(8,128)(2,1)S(1)}, bf16[24,128,128]{2,1,0:T(8,128)(2,1)S(1)}) %tuple.41, (s32[4,24]{1,0:T(4,128)S(1)}, ...), branch_computations={%region_8.9_spmd, %region_9.10_spmd, %region_10.11_spmd} | conditional | flops 555223808 | bytes 75244104 | solution.py:94
  11.0 4.9 %collective-permute-start = (bf16[8,128,128]{2,1,0:T(8,128)(2,1)S(1)}, bf16[8,128,128]{2,1,0:T(8,128)(2,1)S(1)}, u32[]{:S(2)}, u32[]{:S(2)}) collective-permute-start(bf16[8,128,128]{2,1,0:T(8,128)(2,1)S(1)} %slice.23), channel_id=1, source_target_pairs={{0,8},{8,16},{16,24},{1,9},{9,17},{17,25},{2,10},{10,18},{18,26},{... | collective-permute-start | bytes 786440 | tf_op jit(solution)/shard_map/cond/branch_0_fun/ppermute | solution.py:39
  15.9 1.3 %collective-permute-start.3 = (bf16[8,128,128]{2,1,0:T(8,128)(2,1)S(1)}, bf16[8,128,128]{2,1,0:T(8,128)(2,1)}, u32[]{:S(2)}, u32[]{:S(2)}) collective-permute-start(bf16[8,128,128]{2,1,0:T(8,128)(2,1)S(1)} %slice.23), channel_id=1, source_target_pairs={{8,0},{16,8},{24,16},{9,1},{17,9},{25,17},{10,2},{18,10},{26,18},{... | collective-permute-start | bytes 786440 | tf_op jit(solution)/shard_map/cond/branch_0_fun/ppermute | solution.py:40
  17.2 4.2 %collective-permute-done = bf16[8,128,128]{2,1,0:T(8,128)(2,1)S(1)} collective-permute-done((bf16[8,128,128]{2,1,0:T(8,128)(2,1)S(1)}, bf16[8,128,128]{2,1,0:T(8,128)(2,1)S(1)}, u32[]{:S(2)}, u32[]{:S(2)}) %collective-permute-start) | collective-permute-done | bytes 262176 | tf_op jit(solution)/shard_map/cond/branch_0_fun/ppermute | solution.py:39
  21.4 5.1 %collective-permute-start.1 = (bf16[8,128,128]{2,1,0:T(8,128)(2,1)S(1)}, bf16[8,128,128]{2,1,0:T(8,128)(2,1)}, u32[]{:S(2)}, u32[]{:S(2)}) collective-permute-start(bf16[8,128,128]{2,1,0:T(8,128)(2,1)S(1)} %collective-permute-done), channel_id=1, source_target_pairs={{0,8},{8,16},{16,24},{1,9},{9,17},{17,25},{2,10},{10,18},{18,26},{... | collective-permute-start | bytes 786440 | tf_op jit(solution)/shard_map/cond/branch_0_fun/ppermute | solution.py:39
  27.6 1.3 %collective-permute-start.4 = (bf16[8,128,128]{2,1,0:T(8,128)(2,1)}, bf16[8,128,128]{2,1,0:T(8,128)(2,1)}, u32[]{:S(2)}, u32[]{:S(2)}) collective-permute-start(bf16[8,128,128]{2,1,0:T(8,128)(2,1)} %collective-permute-done.3), channel_id=1, source_target_pairs={{8,0},{16,8},{24,16},{9,1},{17,9},{25,17},{10,2},{18,10},{26,18},{... | collective-permute-start | bytes 786440 | tf_op jit(solution)/shard_map/cond/branch_0_fun/ppermute | solution.py:40
  28.9 1.6 %collective-permute-done.1 = bf16[8,128,128]{2,1,0:T(8,128)(2,1)} collective-permute-done((bf16[8,128,128]{2,1,0:T(8,128)(2,1)S(1)}, bf16[8,128,128]{2,1,0:T(8,128)(2,1)}, u32[]{:S(2)}, u32[]{:S(2)}) %collective-permute-start.1) | collective-permute-done | bytes 262176 | tf_op jit(solution)/shard_map/cond/branch_0_fun/ppermute | solution.py:39
  30.5 5.2 %collective-permute-start.2 = (bf16[8,128,128]{2,1,0:T(8,128)(2,1)}, bf16[8,128,128]{2,1,0:T(8,128)(2,1)}, u32[]{:S(2)}, u32[]{:S(2)}) collective-permute-start(bf16[8,128,128]{2,1,0:T(8,128)(2,1)} %collective-permute-done.1), channel_id=1, source_target_pairs={{0,8},{8,16},{16,24},{1,9},{9,17},{17,25},{2,10},{10,18},{18,26},{... | collective-permute-start | bytes 786440 | tf_op jit(solution)/shard_map/cond/branch_0_fun/ppermute | solution.py:39
  36.7 1.3 %collective-permute-start.5 = (bf16[8,128,128]{2,1,0:T(8,128)(2,1)}, bf16[8,128,128]{2,1,0:T(8,128)(2,1)S(1)}, u32[]{:S(2)}, u32[]{:S(2)}) collective-permute-start(bf16[8,128,128]{2,1,0:T(8,128)(2,1)} %collective-permute-done.4), channel_id=1, source_target_pairs={{8,0},{16,8},{24,16},{9,1},{17,9},{25,17},{10,2},{18,10},{26,18},{... | collective-permute-start | bytes 786440 | tf_op jit(solution)/shard_map/cond/branch_0_fun/ppermute | solution.py:40
  38.0 1.1 %collective-permute-done.2 = bf16[8,128,128]{2,1,0:T(8,128)(2,1)} collective-permute-done((bf16[8,128,128]{2,1,0:T(8,128)(2,1)}, bf16[8,128,128]{2,1,0:T(8,128)(2,1)}, u32[]{:S(2)}, u32[]{:S(2)}) %collective-permute-start.2) | collective-permute-done | bytes 262176 | tf_op jit(solution)/shard_map/cond/branch_0_fun/ppermute | solution.py:39
  39.2 1.0 %constant_dynamic-update-slice_fusion.6 = bf16[56,128,128]{2,1,0:T(8,128)(2,1)S(1)} fusion(bf16[8,128,128]{2,1,0:T(8,128)(2,1)} %collective-permute-done.2), kind=kLoop, calls=%fused_computation.17 | loop fusion | bytes 524288 | tf_op jit(solution)/shard_map/cond
  40.1 1.0 %constant_dynamic-update-slice_fusion.5 = bf16[56,128,128]{2,1,0:T(8,128)(2,1)S(1)} fusion(bf16[56,128,128]{2,1,0:T(8,128)(2,1)S(1)} %constant_dynamic-update-slice_fusion.6, bf16[8,128,128]{2,1,0:T(8,128)(2,1)} %collective-permute-done.1), kind=kLoop, calls=%fused_computation.16 | loop fusion | bytes 524288 | tf_op jit(solution)/shard_map/cond
  41.2 1.0 %constant_dynamic-update-slice_fusion.2 = bf16[56,128,128]{2,1,0:T(8,128)(2,1)S(1)} fusion(bf16[56,128,128]{2,1,0:T(8,128)(2,1)S(1)} %constant_dynamic-update-slice_fusion.3, bf16[8,128,128]{2,1,0:T(8,128)(2,1)} %collective-permute-done.3), kind=kLoop, calls=%fused_computation.13 | loop fusion | bytes 524288 | tf_op jit(solution)/shard_map/cond
  42.2 1.0 %constant_dynamic-update-slice_fusion.1 = bf16[56,128,128]{2,1,0:T(8,128)(2,1)S(1)} fusion(bf16[56,128,128]{2,1,0:T(8,128)(2,1)S(1)} %constant_dynamic-update-slice_fusion.2, bf16[8,128,128]{2,1,0:T(8,128)(2,1)} %collective-permute-done.4), kind=kLoop, calls=%fused_computation.12 | loop fusion | bytes 524288 | tf_op jit(solution)/shard_map/cond
  43.2 2.0 %collective-permute-done.5 = bf16[8,128,128]{2,1,0:T(8,128)(2,1)S(1)} collective-permute-done((bf16[8,128,128]{2,1,0:T(8,128)(2,1)}, bf16[8,128,128]{2,1,0:T(8,128)(2,1)S(1)}, u32[]{:S(2)}, u32[]{:S(2)}) %collective-permute-start.5) | collective-permute-done | bytes 262176 | tf_op jit(solution)/shard_map/cond/branch_0_fun/ppermute | solution.py:40
  45.7 2.0 %fusion = f32[8,128,128]{2,0,1:T(8,128)S(1)} fusion(f32[32,128,128]{2,1,0:T(8,128)S(1)} %fusion.2, s32[32]{0:T(128)S(1)} %eq.76, pred[32]{0:T(512)(128)(4,1)S(1)} %and.74), kind=kOutput, calls=%fused_computation.4 | convolution fusion | flops 50332160 | bytes 2621600 | tf_op jit(solution)/shard_map/cond/branch_0_fun/ts,src->trc/dot_general | solution.py:57
  48.5 1.5 %collective-permute-done.18 = f32[4,128,128]{2,0,1:T(4,128)S(1)} collective-permute-done((f32[4,128,128]{2,0,1:T(4,128)S(1)}, f32[4,128,128]{2,0,1:T(4,128)S(1)}, u32[]{:S(2)}, u32[]{:S(2)}) %collective-permute-start.18) | collective-permute-done | bytes 262176 | tf_op jit(solution)/shard_map/ppermute | solution.py:17
  50.3 1.6 %collective-permute-start.19 = (f32[2,128,128]{2,1,0:T(8,128)S(1)}, f32[2,128,128]{2,1,0:T(8,128)S(1)}, u32[]{:S(2)}, u32[]{:S(2)}) collective-permute-start(f32[2,128,128]{2,1,0:T(8,128)S(1)} %bitcast.72), channel_id=1, source_target_pairs={{0,2},{1,3},{2,0},{3,1},{4,6},{5,7},{6,4},{7,5},{8,10},{9,11},{10,... | collective-permute-start | bytes 393224 | tf_op jit(solution)/shard_map/ppermute | solution.py:17
  53.8 2.1 %collective-permute-done.19 = f32[2,128,128]{2,1,0:T(8,128)S(1)} collective-permute-done((f32[2,128,128]{2,1,0:T(8,128)S(1)}, f32[2,128,128]{2,1,0:T(8,128)S(1)}, u32[]{:S(2)}, u32[]{:S(2)}) %collective-permute-start.19) | collective-permute-done | bytes 131104 | tf_op jit(solution)/shard_map/ppermute | solution.py:17
  56.0 1.6 %collective-permute-start.20 = (f32[1,128,128]{2,1,0:T(8,128)S(1)}, f32[1,128,128]{2,1,0:T(8,128)S(1)}, u32[]{:S(2)}, u32[]{:S(2)}) collective-permute-start(f32[1,128,128]{2,1,0:T(8,128)S(1)} %constant_dynamic-slice_fusion.6), channel_id=1, source_target_pairs={{0,4},{1,5},{2,6},{3,7},{4,0},{5,1},{6,2},{7,3},{8,12},{9,13},{10,... | collective-permute-start | bytes 196616 | tf_op jit(solution)/shard_map/ppermute | solution.py:17
  57.6 2.7 %collective-permute-done.20 = f32[1,128,128]{2,1,0:T(8,128)S(1)} collective-permute-done((f32[1,128,128]{2,1,0:T(8,128)S(1)}, f32[1,128,128]{2,1,0:T(8,128)S(1)}, u32[]{:S(2)}, u32[]{:S(2)}) %collective-permute-start.20) | collective-permute-done | bytes 65568 | tf_op jit(solution)/shard_map/ppermute | solution.py:17
  60.3 0.9 %bitcast_select_fusion = bf16[1024,128]{1,0:T(8,128)(2,1)} fusion(pred[1024]{0:T(1024)(128)(4,1)S(1)} %broadcast_bitcast_fusion.1, bf16[128,128]{1,0:T(8,128)(2,1)S(1)} %fusion.47), kind=kLoop, calls=%fused_computation.78 | loop fusion | flops 131072 | bytes 295936 | tf_op jit(solution)/shard_map/jit(_where)/select_n | solution.py:106
  (59 shorter events, 11.2 us)
Async XLA Ops:
  0.0 10.1 %copy-start = (bf16[1536,256]{1,0:T(8,128)(2,1)S(1)}, bf16[1536,256]{1,0:T(8,128)(2,1)}, u32[]{:S(2)}) copy-start(bf16[1536,256]{1,0:T(8,128)(2,1)} %param.9) | copy-start | bytes 2359300
  10.9 41.0 %copy-start.7 = (s32[8]{0:T(128)S(1)}, s32[8]{0:T(128)}, u32[]{:S(2)}) copy-start(s32[8]{0:T(128)} %param.12) | copy-start | bytes 100
  10.9 41.0 %copy-start.8 = (s32[8]{0:T(128)S(1)}, s32[8]{0:T(128)}, u32[]{:S(2)}) copy-start(s32[8]{0:T(128)} %param.10) | copy-start | bytes 100
  11.0 10.5 %collective-permute-start = (bf16[8,128,128]{2,1,0:T(8,128)(2,1)S(1)}, bf16[8,128,128]{2,1,0:T(8,128)(2,1)S(1)}, u32[]{:S(2)}, u32[]{:S(2)}) collective-permute-start(bf16[8,128,128]{2,1,0:T(8,128)(2,1)S(1)} %slice.23), channel_id=1, source_target_pairs={{0,8},{8,16},{16,24},{1,9},{9,17},{17,25},{2,10},{10,18},{18,26},{... | collective-permute-start | bytes 786440 | tf_op jit(solution)/shard_map/cond/branch_0_fun/ppermute | solution.py:39
  15.9 11.7 %collective-permute-start.3 = (bf16[8,128,128]{2,1,0:T(8,128)(2,1)S(1)}, bf16[8,128,128]{2,1,0:T(8,128)(2,1)}, u32[]{:S(2)}, u32[]{:S(2)}) collective-permute-start(bf16[8,128,128]{2,1,0:T(8,128)(2,1)S(1)} %slice.23), channel_id=1, source_target_pairs={{8,0},{16,8},{24,16},{9,1},{17,9},{25,17},{10,2},{18,10},{26,18},{... | collective-permute-start | bytes 786440 | tf_op jit(solution)/shard_map/cond/branch_0_fun/ppermute | solution.py:40
  21.4 14.3 %copy-start.5 = (bf16[8,128,128]{2,1,0:T(8,128)(2,1)}, bf16[8,128,128]{2,1,0:T(8,128)(2,1)S(1)}, u32[]{:S(2)}) copy-start(bf16[8,128,128]{2,1,0:T(8,128)(2,1)S(1)} %collective-permute-done) | copy-start | bytes 786436 | tf_op jit(solution)/shard_map/cond
  21.4 9.1 %collective-permute-start.1 = (bf16[8,128,128]{2,1,0:T(8,128)(2,1)S(1)}, bf16[8,128,128]{2,1,0:T(8,128)(2,1)}, u32[]{:S(2)}, u32[]{:S(2)}) collective-permute-start(bf16[8,128,128]{2,1,0:T(8,128)(2,1)S(1)} %collective-permute-done), channel_id=1, source_target_pairs={{0,8},{8,16},{16,24},{1,9},{9,17},{17,25},{2,10},{10,18},{18,26},{... | collective-permute-start | bytes 786440 | tf_op jit(solution)/shard_map/cond/branch_0_fun/ppermute | solution.py:39
  27.6 9.1 %collective-permute-start.4 = (bf16[8,128,128]{2,1,0:T(8,128)(2,1)}, bf16[8,128,128]{2,1,0:T(8,128)(2,1)}, u32[]{:S(2)}, u32[]{:S(2)}) collective-permute-start(bf16[8,128,128]{2,1,0:T(8,128)(2,1)} %collective-permute-done.3), channel_id=1, source_target_pairs={{8,0},{16,8},{24,16},{9,1},{17,9},{25,17},{10,2},{18,10},{26,18},{... | collective-permute-start | bytes 786440 | tf_op jit(solution)/shard_map/cond/branch_0_fun/ppermute | solution.py:40
  30.5 8.7 %collective-permute-start.2 = (bf16[8,128,128]{2,1,0:T(8,128)(2,1)}, bf16[8,128,128]{2,1,0:T(8,128)(2,1)}, u32[]{:S(2)}, u32[]{:S(2)}) collective-permute-start(bf16[8,128,128]{2,1,0:T(8,128)(2,1)} %collective-permute-done.1), channel_id=1, source_target_pairs={{0,8},{8,16},{16,24},{1,9},{9,17},{17,25},{2,10},{10,18},{18,26},{... | collective-permute-start | bytes 786440 | tf_op jit(solution)/shard_map/cond/branch_0_fun/ppermute | solution.py:39
  35.7 5.4 %copy-start.6 = (bf16[8,128,128]{2,1,0:T(8,128)(2,1)S(1)}, bf16[8,128,128]{2,1,0:T(8,128)(2,1)}, u32[]{:S(2)}) copy-start(bf16[8,128,128]{2,1,0:T(8,128)(2,1)} %copy-done.5) | copy-start | bytes 786436 | tf_op jit(solution)/shard_map/cond
  36.7 8.5 %collective-permute-start.5 = (bf16[8,128,128]{2,1,0:T(8,128)(2,1)}, bf16[8,128,128]{2,1,0:T(8,128)(2,1)S(1)}, u32[]{:S(2)}, u32[]{:S(2)}) collective-permute-start(bf16[8,128,128]{2,1,0:T(8,128)(2,1)} %collective-permute-done.4), channel_id=1, source_target_pairs={{8,0},{16,8},{24,16},{9,1},{17,9},{25,17},{10,2},{18,10},{26,18},{... | collective-permute-start | bytes 786440 | tf_op jit(solution)/shard_map/cond/branch_0_fun/ppermute | solution.py:40
  48.4 1.6 %collective-permute-start.18 = (f32[4,128,128]{2,0,1:T(4,128)S(1)}, f32[4,128,128]{2,0,1:T(4,128)S(1)}, u32[]{:S(2)}, u32[]{:S(2)}) collective-permute-start(f32[4,128,128]{2,0,1:T(4,128)S(1)} %bitcast.71), channel_id=1, source_target_pairs={{0,1},{1,0},{2,3},{3,2},{4,5},{5,4},{6,7},{7,6},{8,9},{9,8},{10,11... | collective-permute-start | bytes 786440 | tf_op jit(solution)/shard_map/ppermute | solution.py:17
  50.3 5.6 %collective-permute-start.19 = (f32[2,128,128]{2,1,0:T(8,128)S(1)}, f32[2,128,128]{2,1,0:T(8,128)S(1)}, u32[]{:S(2)}, u32[]{:S(2)}) collective-permute-start(f32[2,128,128]{2,1,0:T(8,128)S(1)} %bitcast.72), channel_id=1, source_target_pairs={{0,2},{1,3},{2,0},{3,1},{4,6},{5,7},{6,4},{7,5},{8,10},{9,11},{10,... | collective-permute-start | bytes 393224 | tf_op jit(solution)/shard_map/ppermute | solution.py:17
  56.0 4.3 %collective-permute-start.20 = (f32[1,128,128]{2,1,0:T(8,128)S(1)}, f32[1,128,128]{2,1,0:T(8,128)S(1)}, u32[]{:S(2)}, u32[]{:S(2)}) collective-permute-start(f32[1,128,128]{2,1,0:T(8,128)S(1)} %constant_dynamic-slice_fusion.6), channel_id=1, source_target_pairs={{0,4},{1,5},{2,6},{3,7},{4,0},{5,1},{6,2},{7,3},{8,12},{9,13},{10,... | collective-permute-start | bytes 196616 | tf_op jit(solution)/shard_map/ppermute | solution.py:17
where the time goes:
time: 61.7 us; the launch traced here: 61.2 us
  starting transfers between devices  22.3 us (36%)
  waiting for transfers between devices  15.4 us (25%)
  local copies, waits for them, and re-layouts  10 us (16%)
  other arithmetic  9.11 us (15%)
  matrix products  2.45 us (4%)
  between operations  1.53 us (2%)
    ppermute x3, starting transfers between devices, line_gather(): from_left = lax.ppermute(from_left, axis, rightward)  15.2 us
    ppermute x3, waiting for transfers between devices, line_gather(): from_left = lax.ppermute(from_left, axis, rightward)  6.93 us
    ppermute x3, waiting for transfers between devices, halving_reduce_scatter(): parts = keep + lax.ppermute(send, axis, perm)  6.26 us
    cond x10, local copies, waits for them, and re-layouts  4.01 us
    ppermute x3, starting transfers between devices, line_gather(): from_right = lax.ppermute(from_right, axis, leftward)  3.86 us
    ppermute x3, starting transfers between devices, halving_reduce_scatter(): parts = keep + lax.ppermute(send, axis, perm)  3.21 us
    reduce_sum x1, other arithmetic, on_device(): jnp.sum(jnp.where(pick[:, None, :], lam3, jnp.zeros((), lam.dtype)), axis=0)  2.7 us
    ppermute x3, waiting for transfers between devices, line_gather(): from_right = lax.ppermute(from_right, axis, leftward)  2.25 us
  transfers between devices with their start and end apart: 9, of which 8 were waited for; matrix products, arithmetic and copies ran while one was open for 13% of the time, Pallas kernels for 0%

commit v1 on v0

--- a/solution.py
+++ b/solution.py
@@ -31,15 +31,10 @@
 def line_gather(x, axis):
     n = lax.axis_size(axis)
     me = lax.axis_index(axis)
-    rightward = [(a, a + 1) for a in range(n - 1)]
-    leftward = [(a, a - 1) for a in range(1, n)]
     lefts, rights = [], []
-    from_left, from_right = x, x
-    for _ in range(1, n):
-        from_left = lax.ppermute(from_left, axis, rightward)
-        from_right = lax.ppermute(from_right, axis, leftward)
-        lefts.append(from_left)
-        rights.append(from_right)
+    for dist in range(1, n):
+        lefts.append(lax.ppermute(x, axis, [(a, a + dist) for a in range(n - dist)]))
+        rights.append(lax.ppermute(x, axis, [(a, a - dist) for a in range(dist, n)]))
     line = jnp.concatenate(lefts[::-1] + [x] + rights)
     return lax.dynamic_slice_in_dim(line, (n - 1 - me) * x.shape[0], n * x.shape[0])
 

time: 61.7 us -> 64.4 us (1.044)
  waiting for transfers between devices: 15.4 us -> 21.7 us
  starting transfers between devices: 22.3 us -> 19.2 us
    ppermute x6, waiting for transfers between devices: 9.19 us -> 16.1 us  [the longest x3 11.5 us: line_gather(): lax.ppermute(x, axis, [(a, a - dist) for a in range(dist, n)])]
    ppermute x6, starting transfers between devices: 19.1 us -> 16 us  [the longest x3 12.1 us: line_gather(): lax.ppermute(x, axis, [(a, a + dist) for a in range(n - dist)])]
    another operation x1, other arithmetic: 0.7 us -> 1.37 us  [on_device(): row_of = jnp.argmax(occ_sym[None, :] == ab_sym[:, None], axis=1)]
    ppermute x3, waiting for transfers between devices: 6.26 us -> 5.61 us  [halving_reduce_scatter(): parts = keep + lax.ppermute(send, axis, perm)]
    cond x10 -> x6, local copies, waits for them, and re-layouts: 4.01 us -> 3.99 us
  transfers between devices with their start and end apart: 9 -> 9, of which waited for: 8 -> 6; matrix products, arithmetic and copies ran while one was open for 13% -> 12% of each run, Pallas kernels for 0% -> 0%
where the time goes in v1:
time: 64.4 us; the launch traced here: 64 us
  waiting for transfers between devices  21.7 us (34%)
  starting transfers between devices  19.2 us (30%)
  local copies, waits for them, and re-layouts  9.39 us (15%)
  other arithmetic  9.32 us (14%)
  matrix products  2.46 us (4%)
  between operations  1.53 us (2%)
    ppermute x3, starting transfers between devices, line_gather(): lax.ppermute(x, axis, [(a, a + dist) for a in range(n - dist)])  12.1 us
    ppermute x3, waiting for transfers between devices, line_gather(): lax.ppermute(x, axis, [(a, a - dist) for a in range(dist, n)])  11.5 us
    ppermute x3, waiting for transfers between devices, halving_reduce_scatter(): parts = keep + lax.ppermute(send, axis, perm)  5.61 us
    ppermute x3, waiting for transfers between devices, line_gather(): lax.ppermute(x, axis, [(a, a + dist) for a in range(n - dist)])  4.58 us
    cond x6, local copies, waits for them, and re-layouts  3.99 us
    ppermute x3, starting transfers between devices, line_gather(): lax.ppermute(x, axis, [(a, a - dist) for a in range(dist, n)])  3.86 us
    ppermute x3, starting transfers between devices, halving_reduce_scatter(): parts = keep + lax.ppermute(send, axis, perm)  3.2 us
    reduce_sum x1, other arithmetic, on_device(): jnp.sum(jnp.where(pick[:, None, :], lam3, jnp.zeros((), lam.dtype)), axis=0)  2.7 us
  transfers between devices with their start and end apart: 9, of which 6 were waited for; matrix products, arithmetic and copies ran while one was open for 12% of the time, Pallas kernels for 0%

profile of v1, /device:TPU:0, one launch (start us, length us, event | category | flops | bytes accessed | tf_op | source)
XLA Modules:
  0.0 64.0 jit_solution(2866560630035518168)
XLA Ops:
  5.0 1.4 %iota_reduce_fusion = (pred[12]{0:T(512)(128)(4,1)}, s32[12]{0:T(128)S(1)}) fusion(s32[12]{0:T(128)} %param.11, s32[8]{0:T(128)} %param.10), kind=kLoop, calls=%fused_computation.92 | loop fusion | flops 684 | bytes 140 | tf_op jit(solution)/shard_map/on_device/reduce | solution.py:82
  6.6 2.7 %select_reduce_fusion = bf16[128,1536]{1,0:T(8,128)(2,1)S(1)} fusion(bf16[8,128,1536]{2,1,0:T(8,128)(2,1)} %bitcast.65, pred[8,1536]{1,0:T(8,128)(4,1)S(1)} %broadcast_bitcast_fusion), kind=kLoop, calls=%fused_computation.76 | loop fusion | flops 2949120 | bytes 3551232 | tf_op jit(solution)/shard_map/reduce_sum | solution.py:85
  10.4 40.2 %conditional.1 = (f32[4,2,128,128]{3,1,0,2:T(2,128)S(1)}) conditional(s32[]{:T(128)} %clamp.3, (s32[4,24]{1,0:T(4,128)S(1)}, pred[4,24]{1,0:T(4,128)(4,1)S(1)}, s32[4,24]{1,0:T(4,128)S(1)}, bf16[12,128,128]{1,2,0:T(8,128)(2,1)S(1)}, bf16[24,128,128]{2,1,0:T(8,128)(2,1)S(1)}) %tuple.41, (s32[4,24]{1,0:T(4,128)S(1)}, ...), branch_computations={%region_8.9_spmd, %region_9.10_spmd, %region_10.11_spmd} | conditional | flops 555223808 | bytes 68952592 | solution.py:89
  10.5 7.7 %collective-permute-start = (bf16[8,128,128]{2,1,0:T(8,128)(2,1)S(1)}, bf16[8,128,128]{2,1,0:T(8,128)(2,1)}, u32[]{:S(2)}, u32[]{:S(2)}) collective-permute-start(bf16[8,128,128]{2,1,0:T(8,128)(2,1)S(1)} %slice.23), channel_id=1, source_target_pairs={{0,24},{1,25},{2,26},{3,27},{4,28},{5,29},{6,30},{7,31}} | collective-permute-start | bytes 786440 | tf_op jit(solution)/shard_map/cond/branch_0_fun/ppermute | solution.py:36
  18.1 2.0 %collective-permute-start.1 = (bf16[8,128,128]{2,1,0:T(8,128)(2,1)S(1)}, bf16[8,128,128]{2,1,0:T(8,128)(2,1)}, u32[]{:S(2)}, u32[]{:S(2)}) collective-permute-start(bf16[8,128,128]{2,1,0:T(8,128)(2,1)S(1)} %slice.23), channel_id=1, source_target_pairs={{0,16},{8,24},{1,17},{9,25},{2,18},{10,26},{3,19},{11,27},{4,20},{... | collective-permute-start | bytes 786440 | tf_op jit(solution)/shard_map/cond/branch_0_fun/ppermute | solution.py:36
  20.1 2.5 %collective-permute-start.2 = (bf16[8,128,128]{2,1,0:T(8,128)(2,1)S(1)}, bf16[8,128,128]{2,1,0:T(8,128)(2,1)}, u32[]{:S(2)}, u32[]{:S(2)}) collective-permute-start(bf16[8,128,128]{2,1,0:T(8,128)(2,1)S(1)} %slice.23), channel_id=1, source_target_pairs={{0,8},{8,16},{16,24},{1,9},{9,17},{17,25},{2,10},{10,18},{18,26},{... | collective-permute-start | bytes 786440 | tf_op jit(solution)/shard_map/cond/branch_0_fun/ppermute | solution.py:36
  22.6 1.3 %collective-permute-start.3 = (bf16[8,128,128]{2,1,0:T(8,128)(2,1)S(1)}, bf16[8,128,128]{2,1,0:T(8,128)(2,1)}, u32[]{:S(2)}, u32[]{:S(2)}) collective-permute-start(bf16[8,128,128]{2,1,0:T(8,128)(2,1)S(1)} %slice.23), channel_id=1, source_target_pairs={{8,0},{16,8},{24,16},{9,1},{17,9},{25,17},{10,2},{18,10},{26,18},{... | collective-permute-start | bytes 786440 | tf_op jit(solution)/shard_map/cond/branch_0_fun/ppermute | solution.py:37
  23.9 1.3 %collective-permute-start.4 = (bf16[8,128,128]{2,1,0:T(8,128)(2,1)S(1)}, bf16[8,128,128]{2,1,0:T(8,128)(2,1)S(1)}, u32[]{:S(2)}, u32[]{:S(2)}) collective-permute-start(bf16[8,128,128]{2,1,0:T(8,128)(2,1)S(1)} %slice.23), channel_id=1, source_target_pairs={{16,0},{24,8},{17,1},{25,9},{18,2},{26,10},{19,3},{27,11},{20,4},{... | collective-permute-start | bytes 786440 | tf_op jit(solution)/shard_map/cond/branch_0_fun/ppermute | solution.py:37
  26.5 1.3 %collective-permute-start.5 = (bf16[8,128,128]{2,1,0:T(8,128)(2,1)S(1)}, bf16[8,128,128]{2,1,0:T(8,128)(2,1)S(1)}, u32[]{:S(2)}, u32[]{:S(2)}) collective-permute-start(bf16[8,128,128]{2,1,0:T(8,128)(2,1)S(1)} %slice.23), channel_id=1, source_target_pairs={{24,0},{25,1},{26,2},{27,3},{28,4},{29,5},{30,6},{31,7}} | collective-permute-start | bytes 786440 | tf_op jit(solution)/shard_map/cond/branch_0_fun/ppermute | solution.py:37
  27.8 1.0 %constant_dynamic-update-slice_fusion.6 = bf16[56,128,128]{2,1,0:T(8,128)(2,1)S(1)} fusion(bf16[8,128,128]{2,1,0:T(8,128)(2,1)} %collective-permute-done), kind=kLoop, calls=%fused_computation.17 | loop fusion | bytes 524288 | tf_op jit(solution)/shard_map/cond
  28.7 1.1 %collective-permute-done.1 = bf16[8,128,128]{2,1,0:T(8,128)(2,1)} collective-permute-done((bf16[8,128,128]{2,1,0:T(8,128)(2,1)S(1)}, bf16[8,128,128]{2,1,0:T(8,128)(2,1)}, u32[]{:S(2)}, u32[]{:S(2)}) %collective-permute-start.1) | collective-permute-done | bytes 262176 | tf_op jit(solution)/shard_map/cond/branch_0_fun/ppermute | solution.py:36
  29.8 1.0 %constant_dynamic-update-slice_fusion.5 = bf16[56,128,128]{2,1,0:T(8,128)(2,1)S(1)} fusion(bf16[56,128,128]{2,1,0:T(8,128)(2,1)S(1)} %constant_dynamic-update-slice_fusion.6, bf16[8,128,128]{2,1,0:T(8,128)(2,1)} %collective-permute-done.1), kind=kLoop, calls=%fused_computation.16 | loop fusion | bytes 524288 | tf_op jit(solution)/shard_map/cond
  30.8 3.5 %collective-permute-done.2 = bf16[8,128,128]{2,1,0:T(8,128)(2,1)} collective-permute-done((bf16[8,128,128]{2,1,0:T(8,128)(2,1)S(1)}, bf16[8,128,128]{2,1,0:T(8,128)(2,1)}, u32[]{:S(2)}, u32[]{:S(2)}) %collective-permute-start.2) | collective-permute-done | bytes 262176 | tf_op jit(solution)/shard_map/cond/branch_0_fun/ppermute | solution.py:36
  34.3 1.0 %constant_dynamic-update-slice_fusion.4 = bf16[56,128,128]{2,1,0:T(8,128)(2,1)S(1)} fusion(bf16[56,128,128]{2,1,0:T(8,128)(2,1)S(1)} %constant_dynamic-update-slice_fusion.5, bf16[8,128,128]{2,1,0:T(8,128)(2,1)} %collective-permute-done.2), kind=kLoop, calls=%fused_computation.15 | loop fusion | bytes 524288 | tf_op jit(solution)/shard_map/cond
  35.4 1.0 %constant_dynamic-update-slice_fusion.2 = bf16[56,128,128]{2,1,0:T(8,128)(2,1)S(1)} fusion(bf16[56,128,128]{2,1,0:T(8,128)(2,1)S(1)} %constant_dynamic-update-slice_fusion.3, bf16[8,128,128]{2,1,0:T(8,128)(2,1)} %collective-permute-done.3), kind=kLoop, calls=%fused_computation.13 | loop fusion | bytes 524288 | tf_op jit(solution)/shard_map/cond
  36.3 11.5 %collective-permute-done.4 = bf16[8,128,128]{2,1,0:T(8,128)(2,1)S(1)} collective-permute-done((bf16[8,128,128]{2,1,0:T(8,128)(2,1)S(1)}, bf16[8,128,128]{2,1,0:T(8,128)(2,1)S(1)}, u32[]{:S(2)}, u32[]{:S(2)}) %collective-permute-start.4) | collective-permute-done | bytes 262176 | tf_op jit(solution)/shard_map/cond/branch_0_fun/ppermute | solution.py:37
  48.5 2.0 %fusion = f32[8,128,128]{2,0,1:T(8,128)S(1)} fusion(f32[32,128,128]{2,1,0:T(8,128)S(1)} %fusion.2, s32[32]{0:T(128)S(1)} %eq.76, pred[32]{0:T(512)(128)(4,1)S(1)} %and.74), kind=kOutput, calls=%fused_computation.4 | convolution fusion | flops 50332160 | bytes 2621600 | tf_op jit(solution)/shard_map/cond/branch_0_fun/ts,src->trc/dot_general | solution.py:52
  51.3 1.5 %collective-permute-done.18 = f32[4,128,128]{2,0,1:T(4,128)S(1)} collective-permute-done((f32[4,128,128]{2,0,1:T(4,128)S(1)}, f32[4,128,128]{2,0,1:T(4,128)S(1)}, u32[]{:S(2)}, u32[]{:S(2)}) %collective-permute-start.18) | collective-permute-done | bytes 262176 | tf_op jit(solution)/shard_map/ppermute | solution.py:17
  53.1 1.5 %collective-permute-start.19 = (f32[2,128,128]{2,1,0:T(8,128)S(1)}, f32[2,128,128]{2,1,0:T(8,128)S(1)}, u32[]{:S(2)}, u32[]{:S(2)}) collective-permute-start(f32[2,128,128]{2,1,0:T(8,128)S(1)} %bitcast.72), channel_id=1, source_target_pairs={{0,2},{1,3},{2,0},{3,1},{4,6},{5,7},{6,4},{7,5},{8,10},{9,11},{10,... | collective-permute-start | bytes 393224 | tf_op jit(solution)/shard_map/ppermute | solution.py:17
  54.6 1.4 %iota_reduce_fusion.1 = (pred[8]{0:T(512)(128)(4,1)}, s32[8]{0:T(128)S(1)}) fusion(s32[8]{0:T(128)} %param.10, s32[8]{0:T(128)} %param.12), kind=kLoop, calls=%fused_computation.93 | loop fusion | flops 456 | bytes 104 | tf_op jit(solution)/shard_map/on_device/reduce | solution.py:64
  57.2 1.4 %collective-permute-done.19 = f32[2,128,128]{2,1,0:T(8,128)S(1)} collective-permute-done((f32[2,128,128]{2,1,0:T(8,128)S(1)}, f32[2,128,128]{2,1,0:T(8,128)S(1)}, u32[]{:S(2)}, u32[]{:S(2)}) %collective-permute-start.19) | collective-permute-done | bytes 131104 | tf_op jit(solution)/shard_map/ppermute | solution.py:17
  58.7 1.6 %collective-permute-start.20 = (f32[1,128,128]{2,1,0:T(8,128)S(1)}, f32[1,128,128]{2,1,0:T(8,128)S(1)}, u32[]{:S(2)}, u32[]{:S(2)}) collective-permute-start(f32[1,128,128]{2,1,0:T(8,128)S(1)} %constant_dynamic-slice_fusion.6), channel_id=1, source_target_pairs={{0,4},{1,5},{2,6},{3,7},{4,0},{5,1},{6,2},{7,3},{8,12},{9,13},{10,... | collective-permute-start | bytes 196616 | tf_op jit(solution)/shard_map/ppermute | solution.py:17
  60.4 2.7 %collective-permute-done.20 = f32[1,128,128]{2,1,0:T(8,128)S(1)} collective-permute-done((f32[1,128,128]{2,1,0:T(8,128)S(1)}, f32[1,128,128]{2,1,0:T(8,128)S(1)}, u32[]{:S(2)}, u32[]{:S(2)}) %collective-permute-start.20) | collective-permute-done | bytes 65568 | tf_op jit(solution)/shard_map/ppermute | solution.py:17
  63.1 0.9 %bitcast_select_fusion = bf16[1024,128]{1,0:T(8,128)(2,1)} fusion(pred[1024]{0:T(1024)(128)(4,1)S(1)} %broadcast_bitcast_fusion.1, bf16[128,128]{1,0:T(8,128)(2,1)S(1)} %fusion.47), kind=kLoop, calls=%fused_computation.78 | loop fusion | flops 131072 | bytes 295936 | tf_op jit(solution)/shard_map/jit(_where)/select_n | solution.py:101
  (51 shorter events, 9.0 us)
Async XLA Ops:
  0.0 9.6 %copy-start = (bf16[1536,256]{1,0:T(8,128)(2,1)S(1)}, bf16[1536,256]{1,0:T(8,128)(2,1)}, u32[]{:S(2)}) copy-start(bf16[1536,256]{1,0:T(8,128)(2,1)} %param.9) | copy-start | bytes 2359300
  10.5 16.0 %collective-permute-start = (bf16[8,128,128]{2,1,0:T(8,128)(2,1)S(1)}, bf16[8,128,128]{2,1,0:T(8,128)(2,1)}, u32[]{:S(2)}, u32[]{:S(2)}) collective-permute-start(bf16[8,128,128]{2,1,0:T(8,128)(2,1)S(1)} %slice.23), channel_id=1, source_target_pairs={{0,24},{1,25},{2,26},{3,27},{4,28},{5,29},{6,30},{7,31}} | collective-permute-start | bytes 786440 | tf_op jit(solution)/shard_map/cond/branch_0_fun/ppermute | solution.py:36
  18.1 11.7 %collective-permute-start.1 = (bf16[8,128,128]{2,1,0:T(8,128)(2,1)S(1)}, bf16[8,128,128]{2,1,0:T(8,128)(2,1)}, u32[]{:S(2)}, u32[]{:S(2)}) collective-permute-start(bf16[8,128,128]{2,1,0:T(8,128)(2,1)S(1)} %slice.23), channel_id=1, source_target_pairs={{0,16},{8,24},{1,17},{9,25},{2,18},{10,26},{3,19},{11,27},{4,20},{... | collective-permute-start | bytes 786440 | tf_op jit(solution)/shard_map/cond/branch_0_fun/ppermute | solution.py:36
  20.1 14.2 %collective-permute-start.2 = (bf16[8,128,128]{2,1,0:T(8,128)(2,1)S(1)}, bf16[8,128,128]{2,1,0:T(8,128)(2,1)}, u32[]{:S(2)}, u32[]{:S(2)}) collective-permute-start(bf16[8,128,128]{2,1,0:T(8,128)(2,1)S(1)} %slice.23), channel_id=1, source_target_pairs={{0,8},{8,16},{16,24},{1,9},{9,17},{17,25},{2,10},{10,18},{18,26},{... | collective-permute-start | bytes 786440 | tf_op jit(solution)/shard_map/cond/branch_0_fun/ppermute | solution.py:36
  22.6 12.7 %collective-permute-start.3 = (bf16[8,128,128]{2,1,0:T(8,128)(2,1)S(1)}, bf16[8,128,128]{2,1,0:T(8,128)(2,1)}, u32[]{:S(2)}, u32[]{:S(2)}) collective-permute-start(bf16[8,128,128]{2,1,0:T(8,128)(2,1)S(1)} %slice.23), channel_id=1, source_target_pairs={{8,0},{16,8},{24,16},{9,1},{17,9},{25,17},{10,2},{18,10},{26,18},{... | collective-permute-start | bytes 786440 | tf_op jit(solution)/shard_map/cond/branch_0_fun/ppermute | solution.py:37
  23.9 24.0 %collective-permute-start.4 = (bf16[8,128,128]{2,1,0:T(8,128)(2,1)S(1)}, bf16[8,128,128]{2,1,0:T(8,128)(2,1)S(1)}, u32[]{:S(2)}, u32[]{:S(2)}) collective-permute-start(bf16[8,128,128]{2,1,0:T(8,128)(2,1)S(1)} %slice.23), channel_id=1, source_target_pairs={{16,0},{24,8},{17,1},{25,9},{18,2},{26,10},{19,3},{27,11},{20,4},{... | collective-permute-start | bytes 786440 | tf_op jit(solution)/shard_map/cond/branch_0_fun/ppermute | solution.py:37
  26.5 21.4 %collective-permute-start.5 = (bf16[8,128,128]{2,1,0:T(8,128)(2,1)S(1)}, bf16[8,128,128]{2,1,0:T(8,128)(2,1)S(1)}, u32[]{:S(2)}, u32[]{:S(2)}) collective-permute-start(bf16[8,128,128]{2,1,0:T(8,128)(2,1)S(1)} %slice.23), channel_id=1, source_target_pairs={{24,0},{25,1},{26,2},{27,3},{28,4},{29,5},{30,6},{31,7}} | collective-permute-start | bytes 786440 | tf_op jit(solution)/shard_map/cond/branch_0_fun/ppermute | solution.py:37
  51.1 1.6 %collective-permute-start.18 = (f32[4,128,128]{2,0,1:T(4,128)S(1)}, f32[4,128,128]{2,0,1:T(4,128)S(1)}, u32[]{:S(2)}, u32[]{:S(2)}) collective-permute-start(f32[4,128,128]{2,0,1:T(4,128)S(1)} %bitcast.71), channel_id=1, source_target_pairs={{0,1},{1,0},{2,3},{3,2},{4,5},{5,4},{6,7},{7,6},{8,9},{9,8},{10,11... | collective-permute-start | bytes 786440 | tf_op jit(solution)/shard_map/ppermute | solution.py:17
  53.1 5.6 %collective-permute-start.19 = (f32[2,128,128]{2,1,0:T(8,128)S(1)}, f32[2,128,128]{2,1,0:T(8,128)S(1)}, u32[]{:S(2)}, u32[]{:S(2)}) collective-permute-start(f32[2,128,128]{2,1,0:T(8,128)S(1)} %bitcast.72), channel_id=1, source_target_pairs={{0,2},{1,3},{2,0},{3,1},{4,6},{5,7},{6,4},{7,5},{8,10},{9,11},{10,... | collective-permute-start | bytes 393224 | tf_op jit(solution)/shard_map/ppermute | solution.py:17
  58.7 4.3 %collective-permute-start.20 = (f32[1,128,128]{2,1,0:T(8,128)S(1)}, f32[1,128,128]{2,1,0:T(8,128)S(1)}, u32[]{:S(2)}, u32[]{:S(2)}) collective-permute-start(f32[1,128,128]{2,1,0:T(8,128)S(1)} %constant_dynamic-slice_fusion.6), channel_id=1, source_target_pairs={{0,4},{1,5},{2,6},{3,7},{4,0},{5,1},{6,2},{7,3},{8,12},{9,13},{10,... | collective-permute-start | bytes 196616 | tf_op jit(solution)/shard_map/ppermute | solution.py:17

commit v2 on v0

--- a/solution.py
+++ b/solution.py
@@ -45,7 +45,11 @@
 
 
 def packed_partials(lam_kept, int_kept, order, valid, col_of, col_tiles, cap):
-    received = line_gather(int_kept[:cap], "occ")
+    halves = [int_kept[:cap // 2], int_kept[cap // 2:cap]] if cap > 1 else [int_kept[:cap]]
+    peers = order.shape[0]
+    received = jnp.concatenate(
+        [line_gather(h, "occ").reshape(peers, h.shape[0], *h.shape[1:]) for h in halves], axis=1
+    ).reshape(peers * cap, *int_kept.shape[1:])
     q = order[:, :cap].reshape(-1)
     t = col_of[:, :cap].reshape(-1)
     ok = valid[:, :cap].reshape(-1)

time: 61.7 us -> 71.7 us (1.16); the launches traced: 61.2 us -> 70.4 us
  starting transfers between devices: 22.3 us -> 38.9 us
  waiting for transfers between devices: 15.4 us -> 6.29 us
  local copies, waits for them, and re-layouts: 10 us -> 12.1 us
    ppermute x3 -> x6, starting transfers between devices: 15.2 us -> 28 us  [line_gather(): from_left = lax.ppermute(from_left, axis, rightward)]
    ppermute x3 -> x6, waiting for transfers between devices: 6.93 us -> 0.02 us  [line_gather(): from_left = lax.ppermute(from_left, axis, rightward)]
    ppermute x3 -> x6, starting transfers between devices: 3.86 us -> 7.73 us  [line_gather(): from_right = lax.ppermute(from_right, axis, leftward)]
    cond x10 -> x15, local copies, waits for them, and re-layouts: 4.01 us -> 6.56 us
    ppermute x3 -> x6, waiting for transfers between devices: 2.25 us -> 0.02 us  [line_gather(): from_right = lax.ppermute(from_right, axis, leftward)]
  transfers between devices with their start and end apart: 9 -> 15, of which waited for: 8 -> 3; matrix products, arithmetic and copies ran while one was open for 13% -> 14% of each run, Pallas kernels for 0% -> 0%
where the time goes in v2:
time: 71.7 us; the launch traced here: 70.4 us
  starting transfers between devices  38.9 us (54%)
  local copies, waits for them, and re-layouts  12.1 us (17%)
  other arithmetic  8.66 us (12%)
  waiting for transfers between devices  6.29 us (9%)
  matrix products  2.45 us (3%)
  between operations  1.55 us (2%)
    ppermute x6, starting transfers between devices, line_gather(): from_left = lax.ppermute(from_left, axis, rightward)  28 us
    ppermute x6, starting transfers between devices, line_gather(): from_right = lax.ppermute(from_right, axis, leftward)  7.73 us
    cond x15, local copies, waits for them, and re-layouts  6.56 us
    ppermute x3, waiting for transfers between devices, halving_reduce_scatter(): parts = keep + lax.ppermute(send, axis, perm)  6.26 us
    ppermute x3, starting transfers between devices, halving_reduce_scatter(): parts = keep + lax.ppermute(send, axis, perm)  3.21 us
    reduce_sum x1, other arithmetic, on_device(): jnp.sum(jnp.where(pick[:, None, :], lam3, jnp.zeros((), lam.dtype)), axis=0)  2.7 us
    dot_general x1, matrix products, packed_partials(): jnp.einsum('ts,src->trc', onehot.astype(jnp.float32), products, precision...  1.96 us
    eq x6, local copies, waits for them, and re-layouts, on_device(): kept = cd_sym[:, None] == ab_sym[None, :]  1.8 us
  transfers between devices with their start and end apart: 15, of which 3 were waited for; matrix products, arithmetic and copies ran while one was open for 14% of the time, Pallas kernels for 0%

profile of v2, /device:TPU:0, one launch (start us, length us, event | category | flops | bytes accessed | tf_op | source)
XLA Modules:
  0.0 70.4 jit_solution(16097952802541552450)
XLA Ops:
  5.0 1.3 %iota_reduce_fusion = (pred[12]{0:T(512)(128)(4,1)}, s32[12]{0:T(128)S(1)}) fusion(s32[12]{0:T(128)} %param.11, s32[8]{0:T(128)} %param.10), kind=kLoop, calls=%fused_computation.116 | loop fusion | flops 684 | bytes 140 | tf_op jit(solution)/shard_map/on_device/reduce | solution.py:91
  6.5 2.7 %select_reduce_fusion = bf16[128,1536]{1,0:T(8,128)(2,1)S(1)} fusion(bf16[8,128,1536]{2,1,0:T(8,128)(2,1)} %bitcast.82, pred[8,1536]{1,0:T(8,128)(4,1)S(1)} %broadcast_bitcast_fusion), kind=kLoop, calls=%fused_computation.100 | loop fusion | flops 2949120 | bytes 3551232 | tf_op jit(solution)/shard_map/reduce_sum | solution.py:94
  10.4 46.7 %conditional.1 = (f32[4,2,128,128]{3,1,0,2:T(2,128)S(1)}) conditional(s32[]{:T(128)} %clamp.3, (s32[4,24]{1,0:T(4,128)S(1)}, pred[4,24]{1,0:T(4,128)(4,1)S(1)}, s32[4,24]{1,0:T(4,128)S(1)}, bf16[12,128,128]{1,2,0:T(8,128)(2,1)S(1)}, bf16[24,128,128]{2,1,0:T(8,128)(2,1)S(1)}) %tuple.47, (s32[4,24]{1,0:T(4,128)S(1)}, ...), branch_computations={%region_8.9_spmd, %region_9.10_spmd, %region_10.11_spmd} | conditional | flops 556796672 | bytes 86253976 | solution.py:98
  10.4 4.9 %collective-permute-start = (bf16[4,128,128]{2,1,0:T(8,128)(2,1)S(1)}, bf16[4,128,128]{2,1,0:T(8,128)(2,1)S(1)}, u32[]{:S(2)}, u32[]{:S(2)}) collective-permute-start(bf16[4,128,128]{2,1,0:T(8,128)(2,1)S(1)} %get-tuple-element.123), channel_id=1, source_target_pairs={{0,8},{8,16},{16,24},{1,9},{9,17},{17,25},{2,10},{10,18},{18,26},{... | collective-permute-start | bytes 393224 | tf_op jit(solution)/shard_map/cond/branch_0_fun/ppermute | solution.py:39
  15.3 4.1 %collective-permute-start.6 = (bf16[4,128,128]{2,1,0:T(8,128)(2,1)S(1)}, bf16[4,128,128]{2,1,0:T(8,128)(2,1)}, u32[]{:S(2)}, u32[]{:S(2)}) collective-permute-start(bf16[4,128,128]{2,1,0:T(8,128)(2,1)S(1)} %get-tuple-element.124), channel_id=1, source_target_pairs={{0,8},{8,16},{16,24},{1,9},{9,17},{17,25},{2,10},{10,18},{18,26},{... | collective-permute-start | bytes 393224 | tf_op jit(solution)/shard_map/cond/branch_0_fun/ppermute | solution.py:39
  19.5 1.3 %collective-permute-start.9 = (bf16[4,128,128]{2,1,0:T(8,128)(2,1)S(1)}, bf16[4,128,128]{2,1,0:T(8,128)(2,1)}, u32[]{:S(2)}, u32[]{:S(2)}) collective-permute-start(bf16[4,128,128]{2,1,0:T(8,128)(2,1)S(1)} %get-tuple-element.124), channel_id=1, source_target_pairs={{8,0},{16,8},{24,16},{9,1},{17,9},{25,17},{10,2},{18,10},{26,18},{... | collective-permute-start | bytes 393224 | tf_op jit(solution)/shard_map/cond/branch_0_fun/ppermute | solution.py:40
  20.8 1.3 %collective-permute-start.3 = (bf16[4,128,128]{2,1,0:T(8,128)(2,1)S(1)}, bf16[4,128,128]{2,1,0:T(8,128)(2,1)S(1)}, u32[]{:S(2)}, u32[]{:S(2)}) collective-permute-start(bf16[4,128,128]{2,1,0:T(8,128)(2,1)S(1)} %get-tuple-element.123), channel_id=1, source_target_pairs={{8,0},{16,8},{24,16},{9,1},{17,9},{25,17},{10,2},{18,10},{26,18},{... | collective-permute-start | bytes 393224 | tf_op jit(solution)/shard_map/cond/branch_0_fun/ppermute | solution.py:40
  22.1 5.8 %collective-permute-start.1 = (bf16[4,128,128]{2,1,0:T(8,128)(2,1)S(1)}, bf16[4,128,128]{2,1,0:T(8,128)(2,1)}, u32[]{:S(2)}, u32[]{:S(2)}) collective-permute-start(bf16[4,128,128]{2,1,0:T(8,128)(2,1)S(1)} %collective-permute-done), channel_id=1, source_target_pairs={{0,8},{8,16},{16,24},{1,9},{9,17},{17,25},{2,10},{10,18},{18,26},{... | collective-permute-start | bytes 393224 | tf_op jit(solution)/shard_map/cond/branch_0_fun/ppermute | solution.py:39
  28.0 3.9 %collective-permute-start.7 = (bf16[4,128,128]{2,1,0:T(8,128)(2,1)}, bf16[4,128,128]{2,1,0:T(8,128)(2,1)}, u32[]{:S(2)}, u32[]{:S(2)}) collective-permute-start(bf16[4,128,128]{2,1,0:T(8,128)(2,1)} %collective-permute-done.6), channel_id=1, source_target_pairs={{0,8},{8,16},{16,24},{1,9},{9,17},{17,25},{2,10},{10,18},{18,26},{... | collective-permute-start | bytes 393224 | tf_op jit(solution)/shard_map/cond/branch_0_fun/ppermute | solution.py:39
  31.9 1.3 %collective-permute-start.10 = (bf16[4,128,128]{2,1,0:T(8,128)(2,1)}, bf16[4,128,128]{2,1,0:T(8,128)(2,1)}, u32[]{:S(2)}, u32[]{:S(2)}) collective-permute-start(bf16[4,128,128]{2,1,0:T(8,128)(2,1)} %collective-permute-done.9), channel_id=1, source_target_pairs={{8,0},{16,8},{24,16},{9,1},{17,9},{25,17},{10,2},{18,10},{26,18},{... | collective-permute-start | bytes 393224 | tf_op jit(solution)/shard_map/cond/branch_0_fun/ppermute | solution.py:40
  33.2 1.3 %collective-permute-start.4 = (bf16[4,128,128]{2,1,0:T(8,128)(2,1)S(1)}, bf16[4,128,128]{2,1,0:T(8,128)(2,1)}, u32[]{:S(2)}, u32[]{:S(2)}) collective-permute-start(bf16[4,128,128]{2,1,0:T(8,128)(2,1)S(1)} %collective-permute-done.3), channel_id=1, source_target_pairs={{8,0},{16,8},{24,16},{9,1},{17,9},{25,17},{10,2},{18,10},{26,18},{... | collective-permute-start | bytes 393224 | tf_op jit(solution)/shard_map/cond/branch_0_fun/ppermute | solution.py:40
  34.5 5.8 %collective-permute-start.2 = (bf16[4,128,128]{2,1,0:T(8,128)(2,1)}, bf16[4,128,128]{2,1,0:T(8,128)(2,1)}, u32[]{:S(2)}, u32[]{:S(2)}) collective-permute-start(bf16[4,128,128]{2,1,0:T(8,128)(2,1)} %collective-permute-done.1), channel_id=1, source_target_pairs={{0,8},{8,16},{16,24},{1,9},{9,17},{17,25},{2,10},{10,18},{18,26},{... | collective-permute-start | bytes 393224 | tf_op jit(solution)/shard_map/cond/branch_0_fun/ppermute | solution.py:39
  41.6 3.3 %collective-permute-start.8 = (bf16[4,128,128]{2,1,0:T(8,128)(2,1)}, bf16[4,128,128]{2,1,0:T(8,128)(2,1)S(1)}, u32[]{:S(2)}, u32[]{:S(2)}) collective-permute-start(bf16[4,128,128]{2,1,0:T(8,128)(2,1)} %collective-permute-done.7), channel_id=1, source_target_pairs={{0,8},{8,16},{16,24},{1,9},{9,17},{17,25},{2,10},{10,18},{18,26},{... | collective-permute-start | bytes 393224 | tf_op jit(solution)/shard_map/cond/branch_0_fun/ppermute | solution.py:39
  44.9 1.3 %collective-permute-start.11 = (bf16[4,128,128]{2,1,0:T(8,128)(2,1)}, bf16[4,128,128]{2,1,0:T(8,128)(2,1)S(1)}, u32[]{:S(2)}, u32[]{:S(2)}) collective-permute-start(bf16[4,128,128]{2,1,0:T(8,128)(2,1)} %collective-permute-done.10), channel_id=1, source_target_pairs={{8,0},{16,8},{24,16},{9,1},{17,9},{25,17},{10,2},{18,10},{26,18},{... | collective-permute-start | bytes 393224 | tf_op jit(solution)/shard_map/cond/branch_0_fun/ppermute | solution.py:40
  46.2 1.3 %collective-permute-start.5 = (bf16[4,128,128]{2,1,0:T(8,128)(2,1)}, bf16[4,128,128]{2,1,0:T(8,128)(2,1)S(1)}, u32[]{:S(2)}, u32[]{:S(2)}) collective-permute-start(bf16[4,128,128]{2,1,0:T(8,128)(2,1)} %collective-permute-done.4), channel_id=1, source_target_pairs={{8,0},{16,8},{24,16},{9,1},{17,9},{25,17},{10,2},{18,10},{26,18},{... | collective-permute-start | bytes 393224 | tf_op jit(solution)/shard_map/cond/branch_0_fun/ppermute | solution.py:40
  48.4 0.9 %constant_dynamic-update-slice_fusion.5 = bf16[28,128,128]{2,1,0:T(8,128)(2,1)S(1)} fusion(bf16[28,128,128]{2,1,0:T(8,128)(2,1)S(1)} %constant_dynamic-update-slice_fusion.6, bf16[4,128,128]{2,1,0:T(8,128)(2,1)} %collective-permute-done.1), kind=kLoop, calls=%fused_computation.16 | loop fusion | bytes 262144 | tf_op jit(solution)/shard_map/cond
  49.4 0.9 %constant_dynamic-update-slice_fusion.12 = bf16[28,128,128]{2,1,0:T(8,128)(2,1)S(1)} fusion(bf16[28,128,128]{2,1,0:T(8,128)(2,1)S(1)} %constant_dynamic-update-slice_fusion.13, bf16[4,128,128]{2,1,0:T(8,128)(2,1)} %collective-permute-done.7), kind=kLoop, calls=%fused_computation.23 | loop fusion | bytes 262144 | tf_op jit(solution)/shard_map/cond
  50.4 0.9 %constant_dynamic-update-slice_fusion.11 = bf16[28,128,128]{2,1,0:T(8,128)(2,1)S(1)} fusion(bf16[28,128,128]{2,1,0:T(8,128)(2,1)S(1)} %constant_dynamic-update-slice_fusion.12, bf16[4,128,128]{2,1,0:T(8,128)(2,1)} %collective-permute-done.6), kind=kLoop, calls=%fused_computation.22 | loop fusion | bytes 262144 | tf_op jit(solution)/shard_map/cond
  54.9 2.0 %fusion = f32[8,128,128]{2,0,1:T(8,128)S(1)} fusion(f32[32,128,128]{2,1,0:T(8,128)S(1)} %fusion.2, s32[32]{0:T(128)S(1)} %eq.76, pred[32]{0:T(512)(128)(4,1)S(1)} %and.74), kind=kOutput, calls=%fused_computation.4 | convolution fusion | flops 50332160 | bytes 2621600 | tf_op jit(solution)/shard_map/cond/branch_0_fun/ts,src->trc/dot_general | solution.py:61
  57.7 1.5 %collective-permute-done.36 = f32[4,128,128]{2,0,1:T(4,128)S(1)} collective-permute-done((f32[4,128,128]{2,0,1:T(4,128)S(1)}, f32[4,128,128]{2,0,1:T(4,128)S(1)}, u32[]{:S(2)}, u32[]{:S(2)}) %collective-permute-start.36) | collective-permute-done | bytes 262176 | tf_op jit(solution)/shard_map/ppermute | solution.py:17
  59.5 1.6 %collective-permute-start.37 = (f32[2,128,128]{2,1,0:T(8,128)S(1)}, f32[2,128,128]{2,1,0:T(8,128)S(1)}, u32[]{:S(2)}, u32[]{:S(2)}) collective-permute-start(f32[2,128,128]{2,1,0:T(8,128)S(1)} %bitcast.93), channel_id=1, source_target_pairs={{0,2},{1,3},{2,0},{3,1},{4,6},{5,7},{6,4},{7,5},{8,10},{9,11},{10,... | collective-permute-start | bytes 393224 | tf_op jit(solution)/shard_map/ppermute | solution.py:17
  63.0 2.1 %collective-permute-done.37 = f32[2,128,128]{2,1,0:T(8,128)S(1)} collective-permute-done((f32[2,128,128]{2,1,0:T(8,128)S(1)}, f32[2,128,128]{2,1,0:T(8,128)S(1)}, u32[]{:S(2)}, u32[]{:S(2)}) %collective-permute-start.37) | collective-permute-done | bytes 131104 | tf_op jit(solution)/shard_map/ppermute | solution.py:17
  65.2 1.6 %collective-permute-start.38 = (f32[1,128,128]{2,1,0:T(8,128)S(1)}, f32[1,128,128]{2,1,0:T(8,128)S(1)}, u32[]{:S(2)}, u32[]{:S(2)}) collective-permute-start(f32[1,128,128]{2,1,0:T(8,128)S(1)} %constant_dynamic-slice_fusion.12), channel_id=1, source_target_pairs={{0,4},{1,5},{2,6},{3,7},{4,0},{5,1},{6,2},{7,3},{8,12},{9,13},{10,... | collective-permute-start | bytes 196616 | tf_op jit(solution)/shard_map/ppermute | solution.py:17
  66.8 2.7 %collective-permute-done.38 = f32[1,128,128]{2,1,0:T(8,128)S(1)} collective-permute-done((f32[1,128,128]{2,1,0:T(8,128)S(1)}, f32[1,128,128]{2,1,0:T(8,128)S(1)}, u32[]{:S(2)}, u32[]{:S(2)}) %collective-permute-start.38) | collective-permute-done | bytes 65568 | tf_op jit(solution)/shard_map/ppermute | solution.py:17
  (80 shorter events, 14.6 us)
Async XLA Ops:
  0.0 9.5 %copy-start = (bf16[1536,256]{1,0:T(8,128)(2,1)S(1)}, bf16[1536,256]{1,0:T(8,128)(2,1)}, u32[]{:S(2)}) copy-start(bf16[1536,256]{1,0:T(8,128)(2,1)} %param.9) | copy-start | bytes 2359300
  10.4 11.7 %collective-permute-start = (bf16[4,128,128]{2,1,0:T(8,128)(2,1)S(1)}, bf16[4,128,128]{2,1,0:T(8,128)(2,1)S(1)}, u32[]{:S(2)}, u32[]{:S(2)}) collective-permute-start(bf16[4,128,128]{2,1,0:T(8,128)(2,1)S(1)} %get-tuple-element.123), channel_id=1, source_target_pairs={{0,8},{8,16},{16,24},{1,9},{9,17},{17,25},{2,10},{10,18},{18,26},{... | collective-permute-start | bytes 393224 | tf_op jit(solution)/shard_map/cond/branch_0_fun/ppermute | solution.py:39
  15.3 12.7 %collective-permute-start.6 = (bf16[4,128,128]{2,1,0:T(8,128)(2,1)S(1)}, bf16[4,128,128]{2,1,0:T(8,128)(2,1)}, u32[]{:S(2)}, u32[]{:S(2)}) collective-permute-start(bf16[4,128,128]{2,1,0:T(8,128)(2,1)S(1)} %get-tuple-element.124), channel_id=1, source_target_pairs={{0,8},{8,16},{16,24},{1,9},{9,17},{17,25},{2,10},{10,18},{18,26},{... | collective-permute-start | bytes 393224 | tf_op jit(solution)/shard_map/cond/branch_0_fun/ppermute | solution.py:39
  19.5 12.5 %collective-permute-start.9 = (bf16[4,128,128]{2,1,0:T(8,128)(2,1)S(1)}, bf16[4,128,128]{2,1,0:T(8,128)(2,1)}, u32[]{:S(2)}, u32[]{:S(2)}) collective-permute-start(bf16[4,128,128]{2,1,0:T(8,128)(2,1)S(1)} %get-tuple-element.124), channel_id=1, source_target_pairs={{8,0},{16,8},{24,16},{9,1},{17,9},{25,17},{10,2},{18,10},{26,18},{... | collective-permute-start | bytes 393224 | tf_op jit(solution)/shard_map/cond/branch_0_fun/ppermute | solution.py:40
  20.8 12.5 %collective-permute-start.3 = (bf16[4,128,128]{2,1,0:T(8,128)(2,1)S(1)}, bf16[4,128,128]{2,1,0:T(8,128)(2,1)S(1)}, u32[]{:S(2)}, u32[]{:S(2)}) collective-permute-start(bf16[4,128,128]{2,1,0:T(8,128)(2,1)S(1)} %get-tuple-element.123), channel_id=1, source_target_pairs={{8,0},{16,8},{24,16},{9,1},{17,9},{25,17},{10,2},{18,10},{26,18},{... | collective-permute-start | bytes 393224 | tf_op jit(solution)/shard_map/cond/branch_0_fun/ppermute | solution.py:40
  22.1 18.3 %copy-start.5 = (bf16[4,128,128]{2,1,0:T(8,128)(2,1)}, bf16[4,128,128]{2,1,0:T(8,128)(2,1)S(1)}, u32[]{:S(2)}) copy-start(bf16[4,128,128]{2,1,0:T(8,128)(2,1)S(1)} %collective-permute-done) | copy-start | bytes 393220 | tf_op jit(solution)/shard_map/cond
  22.1 12.4 %collective-permute-start.1 = (bf16[4,128,128]{2,1,0:T(8,128)(2,1)S(1)}, bf16[4,128,128]{2,1,0:T(8,128)(2,1)}, u32[]{:S(2)}, u32[]{:S(2)}) collective-permute-start(bf16[4,128,128]{2,1,0:T(8,128)(2,1)S(1)} %collective-permute-done), channel_id=1, source_target_pairs={{0,8},{8,16},{16,24},{1,9},{9,17},{17,25},{2,10},{10,18},{18,26},{... | collective-permute-start | bytes 393224 | tf_op jit(solution)/shard_map/cond/branch_0_fun/ppermute | solution.py:39
  28.0 13.6 %collective-permute-start.7 = (bf16[4,128,128]{2,1,0:T(8,128)(2,1)}, bf16[4,128,128]{2,1,0:T(8,128)(2,1)}, u32[]{:S(2)}, u32[]{:S(2)}) collective-permute-start(bf16[4,128,128]{2,1,0:T(8,128)(2,1)} %collective-permute-done.6), channel_id=1, source_target_pairs={{0,8},{8,16},{16,24},{1,9},{9,17},{17,25},{2,10},{10,18},{18,26},{... | collective-permute-start | bytes 393224 | tf_op jit(solution)/shard_map/cond/branch_0_fun/ppermute | solution.py:39
  31.9 13.0 %collective-permute-start.10 = (bf16[4,128,128]{2,1,0:T(8,128)(2,1)}, bf16[4,128,128]{2,1,0:T(8,128)(2,1)}, u32[]{:S(2)}, u32[]{:S(2)}) collective-permute-start(bf16[4,128,128]{2,1,0:T(8,128)(2,1)} %collective-permute-done.9), channel_id=1, source_target_pairs={{8,0},{16,8},{24,16},{9,1},{17,9},{25,17},{10,2},{18,10},{26,18},{... | collective-permute-start | bytes 393224 | tf_op jit(solution)/shard_map/cond/branch_0_fun/ppermute | solution.py:40
  33.2 13.0 %collective-permute-start.4 = (bf16[4,128,128]{2,1,0:T(8,128)(2,1)S(1)}, bf16[4,128,128]{2,1,0:T(8,128)(2,1)}, u32[]{:S(2)}, u32[]{:S(2)}) collective-permute-start(bf16[4,128,128]{2,1,0:T(8,128)(2,1)S(1)} %collective-permute-done.3), channel_id=1, source_target_pairs={{8,0},{16,8},{24,16},{9,1},{17,9},{25,17},{10,2},{18,10},{26,18},{... | collective-permute-start | bytes 393224 | tf_op jit(solution)/shard_map/cond/branch_0_fun/ppermute | solution.py:40
  34.5 13.0 %collective-permute-start.2 = (bf16[4,128,128]{2,1,0:T(8,128)(2,1)}, bf16[4,128,128]{2,1,0:T(8,128)(2,1)}, u32[]{:S(2)}, u32[]{:S(2)}) collective-permute-start(bf16[4,128,128]{2,1,0:T(8,128)(2,1)} %collective-permute-done.1), channel_id=1, source_target_pairs={{0,8},{8,16},{16,24},{1,9},{9,17},{17,25},{2,10},{10,18},{18,26},{... | collective-permute-start | bytes 393224 | tf_op jit(solution)/shard_map/cond/branch_0_fun/ppermute | solution.py:39
  40.6 8.7 %copy-start.6 = (bf16[4,128,128]{2,1,0:T(8,128)(2,1)S(1)}, bf16[4,128,128]{2,1,0:T(8,128)(2,1)}, u32[]{:S(2)}) copy-start(bf16[4,128,128]{2,1,0:T(8,128)(2,1)} %copy-done.5) | copy-start | bytes 393220 | tf_op jit(solution)/shard_map/cond
  41.6 7.8 %collective-permute-start.8 = (bf16[4,128,128]{2,1,0:T(8,128)(2,1)}, bf16[4,128,128]{2,1,0:T(8,128)(2,1)S(1)}, u32[]{:S(2)}, u32[]{:S(2)}) collective-permute-start(bf16[4,128,128]{2,1,0:T(8,128)(2,1)} %collective-permute-done.7), channel_id=1, source_target_pairs={{0,8},{8,16},{16,24},{1,9},{9,17},{17,25},{2,10},{10,18},{18,26},{... | collective-permute-start | bytes 393224 | tf_op jit(solution)/shard_map/cond/branch_0_fun/ppermute | solution.py:39
  44.9 9.2 %collective-permute-start.11 = (bf16[4,128,128]{2,1,0:T(8,128)(2,1)}, bf16[4,128,128]{2,1,0:T(8,128)(2,1)S(1)}, u32[]{:S(2)}, u32[]{:S(2)}) collective-permute-start(bf16[4,128,128]{2,1,0:T(8,128)(2,1)} %collective-permute-done.10), channel_id=1, source_target_pairs={{8,0},{16,8},{24,16},{9,1},{17,9},{25,17},{10,2},{18,10},{26,18},{... | collective-permute-start | bytes 393224 | tf_op jit(solution)/shard_map/cond/branch_0_fun/ppermute | solution.py:40
  46.2 8.0 %collective-permute-start.5 = (bf16[4,128,128]{2,1,0:T(8,128)(2,1)}, bf16[4,128,128]{2,1,0:T(8,128)(2,1)S(1)}, u32[]{:S(2)}, u32[]{:S(2)}) collective-permute-start(bf16[4,128,128]{2,1,0:T(8,128)(2,1)} %collective-permute-done.4), channel_id=1, source_target_pairs={{8,0},{16,8},{24,16},{9,1},{17,9},{25,17},{10,2},{18,10},{26,18},{... | collective-permute-start | bytes 393224 | tf_op jit(solution)/shard_map/cond/branch_0_fun/ppermute | solution.py:40
  57.1 4.0 %copy-start.7 = (s32[8]{0:T(128)S(1)}, s32[8]{0:T(128)}, u32[]{:S(2)}) copy-start(s32[8]{0:T(128)} %param.12) | copy-start | bytes 100
  57.1 4.0 %copy-start.8 = (s32[8]{0:T(128)S(1)}, s32[8]{0:T(128)}, u32[]{:S(2)}) copy-start(s32[8]{0:T(128)} %param.10) | copy-start | bytes 100
  57.6 1.6 %collective-permute-start.36 = (f32[4,128,128]{2,0,1:T(4,128)S(1)}, f32[4,128,128]{2,0,1:T(4,128)S(1)}, u32[]{:S(2)}, u32[]{:S(2)}) collective-permute-start(f32[4,128,128]{2,0,1:T(4,128)S(1)} %bitcast.92), channel_id=1, source_target_pairs={{0,1},{1,0},{2,3},{3,2},{4,5},{5,4},{6,7},{7,6},{8,9},{9,8},{10,11... | collective-permute-start | bytes 786440 | tf_op jit(solution)/shard_map/ppermute | solution.py:17
  59.5 5.6 %collective-permute-start.37 = (f32[2,128,128]{2,1,0:T(8,128)S(1)}, f32[2,128,128]{2,1,0:T(8,128)S(1)}, u32[]{:S(2)}, u32[]{:S(2)}) collective-permute-start(f32[2,128,128]{2,1,0:T(8,128)S(1)} %bitcast.93), channel_id=1, source_target_pairs={{0,2},{1,3},{2,0},{3,1},{4,6},{5,7},{6,4},{7,5},{8,10},{9,11},{10,... | collective-permute-start | bytes 393224 | tf_op jit(solution)/shard_map/ppermute | solution.py:17
  65.2 4.3 %collective-permute-start.38 = (f32[1,128,128]{2,1,0:T(8,128)S(1)}, f32[1,128,128]{2,1,0:T(8,128)S(1)}, u32[]{:S(2)}, u32[]{:S(2)}) collective-permute-start(f32[1,128,128]{2,1,0:T(8,128)S(1)} %constant_dynamic-slice_fusion.12), channel_id=1, source_target_pairs={{0,4},{1,5},{2,6},{3,7},{4,0},{5,1},{6,2},{7,3},{8,12},{9,13},{10,... | collective-permute-start | bytes 196616 | tf_op jit(solution)/shard_map/ppermute | solution.py:17

commit v3 on v0

--- a/solution.py
+++ b/solution.py
@@ -53,10 +53,13 @@
     products = jnp.einsum(
         "srm,smc->src", lam_tiles, received, preferred_element_type=jnp.float32
     )
-    onehot = (t[None, :] == jnp.arange(col_tiles)[:, None]) & ok[None, :]
-    return jnp.einsum(
-        "ts,src->trc", onehot.astype(jnp.float32), products, precision=lax.Precision.HIGHEST
-    )
+    peers = order.shape[0]
+    own_cols = col_tiles // peers
+    c = (t % own_cols).reshape(peers, 1, cap)
+    mine = (c == jnp.arange(own_cols)[None, :, None]) & ok.reshape(peers, 1, cap)
+    products = products.reshape(peers, 1, cap, *products.shape[1:])
+    partial = jnp.sum(jnp.where(mine[..., None, None], products, 0.0), axis=2)
+    return partial.reshape(col_tiles, *partial.shape[2:])
 
 
 def on_device(lam, integrals, occ_sym, cd_sym, ab_sym):

time: 61.7 us -> 58.4 us (0.947)
  local copies, waits for them, and re-layouts: 10 us -> 5.15 us
  waiting for transfers between devices: 15.4 us -> 19.8 us
  matrix products: 2.45 us -> 0.5 us
  starting transfers between devices: 22.3 us -> 20.8 us
  other arithmetic: 9.11 us -> 9.76 us
    cond x10 -> x6, local copies, waits for them, and re-layouts: 4.01 us -> 0.2 us
    ppermute x3, waiting for transfers between devices: 2.25 us -> 5.45 us  [line_gather(): from_right = lax.ppermute(from_right, axis, leftward)]
    dot_general x1 -> x0, matrix products: 1.96 us -> none  [packed_partials(): jnp.einsum('ts,src->trc', onehot.astype(jnp.float32), products, precision...]
    ppermute x3, waiting for transfers between devices: 6.93 us -> 8.74 us  [line_gather(): from_left = lax.ppermute(from_left, axis, rightward)]
    ppermute x3, starting transfers between devices: 15.2 us -> 13.7 us  [line_gather(): from_left = lax.ppermute(from_left, axis, rightward)]
    and x1 -> x0, local copies, waits for them, and re-layouts: 0.72 us -> none  [packed_partials(): onehot = (t[None, :] == jnp.arange(col_tiles)[:, None]) & ok[None, :]]
    dynamic_slice x3 -> x0, local copies, waits for them, and re-layouts: 0.7 us -> none  [the longest x2 0.46 us: halving_reduce_scatter(): send = lax.dynamic_index_in_dim(pairs, 1 - bit, axis=1, keepdims=False)]
    another operation x1, other arithmetic: 0.7 us -> 1.37 us  [on_device(): row_of = jnp.argmax(occ_sym[None, :] == ab_sym[:, None], axis=1)]
  transfers between devices with their start and end apart: 9 -> 9, of which waited for: 8 -> 7; matrix products, arithmetic and copies ran while one was open for 13% -> 7% of each run, Pallas kernels for 0% -> 0%
where the time goes in v3:
time: 58.4 us; the launch traced here: 58 us
  starting transfers between devices  20.8 us (36%)
  waiting for transfers between devices  19.8 us (34%)
  other arithmetic  9.76 us (17%)
  local copies, waits for them, and re-layouts  5.15 us (9%)
  between operations  1.54 us (3%)
    ppermute x3, starting transfers between devices, line_gather(): from_left = lax.ppermute(from_left, axis, rightward)  13.7 us
    ppermute x3, waiting for transfers between devices, line_gather(): from_left = lax.ppermute(from_left, axis, rightward)  8.74 us
    ppermute x3, waiting for transfers between devices, halving_reduce_scatter(): parts = keep + lax.ppermute(send, axis, perm)  5.59 us
    ppermute x3, waiting for transfers between devices, line_gather(): from_right = lax.ppermute(from_right, axis, leftward)  5.45 us
    ppermute x3, starting transfers between devices, line_gather(): from_right = lax.ppermute(from_right, axis, leftward)  3.88 us
    ppermute x3, starting transfers between devices, halving_reduce_scatter(): parts = keep + lax.ppermute(send, axis, perm)  3.21 us
    reduce_sum x1, other arithmetic, on_device(): jnp.sum(jnp.where(pick[:, None, :], lam3, jnp.zeros((), lam.dtype)), axis=0)  2.69 us
    eq x6, local copies, waits for them, and re-layouts, on_device(): kept = cd_sym[:, None] == ab_sym[None, :]  1.8 us
  transfers between devices with their start and end apart: 9, of which 7 were waited for; matrix products, arithmetic and copies ran while one was open for 7% of the time, Pallas kernels for 0%

profile of v3, /device:TPU:0, one launch (start us, length us, event | category | flops | bytes accessed | tf_op | source)
XLA Modules:
  0.0 58.0 jit_solution(8113802171748581338)
XLA Ops:
  0.0 0.8 %eq.180 = s32[4,2]{1,0:T(4,128)S(1)} reshape(s32[8]{0:T(128)} %param.12) | data formatting | bytes 64 | tf_op jit(solution)/shard_map/eq | solution.py:73
  0.9 0.7 %fusion.41 = s32[4]{0:T(128)S(1)} fusion(s32[4,2]{0,1:T(2,128)S(1)} %copy.29, s32[12]{0:T(128)} %param.11), kind=kLoop, calls=%fused_computation.133 | loop fusion | flops 284 | bytes 96 | tf_op jit(solution)/shard_map/reduce_sum | solution.py:75
  1.7 0.7 %eq.183 = s32[12,2]{1,0:T(8,128)S(1)} broadcast(s32[12]{0:T(128)} %param.11), dimensions={0} | broadcast | bytes 144 | tf_op jit(solution)/shard_map/eq | solution.py:73
  4.9 1.3 %iota_reduce_fusion = (pred[12]{0:T(512)(128)(4,1)}, s32[12]{0:T(128)S(1)}) fusion(s32[12]{0:T(128)} %param.11, s32[8]{0:T(128)} %param.10), kind=kLoop, calls=%fused_computation.135 | loop fusion | flops 684 | bytes 140 | tf_op jit(solution)/shard_map/on_device/reduce | solution.py:90
  6.4 2.7 %select_reduce_fusion.3 = bf16[128,1536]{1,0:T(8,128)(2,1)S(1)} fusion(bf16[8,128,1536]{2,1,0:T(8,128)(2,1)} %bitcast.76, pred[8,1536]{1,0:T(8,128)(4,1)S(1)} %broadcast_bitcast_fusion), kind=kLoop, calls=%fused_computation.120 | loop fusion | flops 2949120 | bytes 3551232 | tf_op jit(solution)/shard_map/reduce_sum | solution.py:93
  9.3 36.0 %conditional.1 = (f32[4,2,128,128]{3,2,1,0:T(8,128)S(1)}) conditional(s32[]{:T(128)} %clamp.3, (s32[4,1]{0,1:T(1,128)S(1)}, s32[4,24]{1,0:T(4,128)S(1)}, s32[4,24]{1,0:T(4,128)S(1)}, pred[4,24,24]{2,1,0:T(8,128)(4,1)S(1)}, s32[4,24]{1,0:T(4,128)S(1)}, /*index=5*/s32[4,24]{1,0:T(4,128)S(1)}, s32[4,24]{1,0:T(4,128)S(1)}, ...), branch_computations={%region_7.10_spmd, %region_10.13_spmd, %region_13.16_spmd} | conditional | flops 411180288 | bytes 81549152 | solution.py:97
  10.5 4.9 %collective-permute-start.6 = (bf16[8,128,128]{2,1,0:T(8,128)(2,1)S(1)}, bf16[8,128,128]{2,1,0:T(8,128)(2,1)S(1)}, u32[]{:S(2)}, u32[]{:S(2)}) collective-permute-start(bf16[8,128,128]{2,1,0:T(8,128)(2,1)S(1)} %slice_select_fusion), channel_id=1, source_target_pairs={{0,8},{8,16},{16,24},{1,9},{9,17},{17,25},{2,10},{10,18},{18,26},{... | collective-permute-start | bytes 786440 | tf_op jit(solution)/shard_map/cond/branch_0_fun/ppermute | solution.py:39
  15.5 1.3 %collective-permute-start.9 = (bf16[8,128,128]{2,1,0:T(8,128)(2,1)S(1)}, bf16[8,128,128]{2,1,0:T(8,128)(2,1)S(1)}, u32[]{:S(2)}, u32[]{:S(2)}) collective-permute-start(bf16[8,128,128]{2,1,0:T(8,128)(2,1)S(1)} %slice_select_fusion), channel_id=1, source_target_pairs={{8,0},{16,8},{24,16},{9,1},{17,9},{25,17},{10,2},{18,10},{26,18},{... | collective-permute-start | bytes 786440 | tf_op jit(solution)/shard_map/cond/branch_0_fun/ppermute | solution.py:40
  16.9 4.1 %collective-permute-done.6 = bf16[8,128,128]{2,1,0:T(8,128)(2,1)S(1)} collective-permute-done((bf16[8,128,128]{2,1,0:T(8,128)(2,1)S(1)}, bf16[8,128,128]{2,1,0:T(8,128)(2,1)S(1)}, u32[]{:S(2)}, u32[]{:S(2)}) %collective-permute-start.6) | collective-permute-done | bytes 262176 | tf_op jit(solution)/shard_map/cond/branch_0_fun/ppermute | solution.py:39
  21.0 4.4 %collective-permute-start.7 = (bf16[8,128,128]{2,1,0:T(8,128)(2,1)S(1)}, bf16[8,128,128]{2,1,0:T(8,128)(2,1)S(1)}, u32[]{:S(2)}, u32[]{:S(2)}) collective-permute-start(bf16[8,128,128]{2,1,0:T(8,128)(2,1)S(1)} %collective-permute-done.6), channel_id=1, source_target_pairs={{0,8},{8,16},{16,24},{1,9},{9,17},{17,25},{2,10},{10,18},{18,26},{... | collective-permute-start | bytes 786440 | tf_op jit(solution)/shard_map/cond/branch_0_fun/ppermute | solution.py:39
  25.5 1.3 %collective-permute-start.10 = (bf16[8,128,128]{2,1,0:T(8,128)(2,1)S(1)}, bf16[8,128,128]{2,1,0:T(8,128)(2,1)S(1)}, u32[]{:S(2)}, u32[]{:S(2)}) collective-permute-start(bf16[8,128,128]{2,1,0:T(8,128)(2,1)S(1)} %collective-permute-done.9), channel_id=1, source_target_pairs={{8,0},{16,8},{24,16},{9,1},{17,9},{25,17},{10,2},{18,10},{26,18},{... | collective-permute-start | bytes 786440 | tf_op jit(solution)/shard_map/cond/branch_0_fun/ppermute | solution.py:40
  26.8 3.3 %collective-permute-done.7 = bf16[8,128,128]{2,1,0:T(8,128)(2,1)S(1)} collective-permute-done((bf16[8,128,128]{2,1,0:T(8,128)(2,1)S(1)}, bf16[8,128,128]{2,1,0:T(8,128)(2,1)S(1)}, u32[]{:S(2)}, u32[]{:S(2)}) %collective-permute-start.7) | collective-permute-done | bytes 262176 | tf_op jit(solution)/shard_map/cond/branch_0_fun/ppermute | solution.py:39
  30.1 4.4 %collective-permute-start.8 = (bf16[8,128,128]{2,1,0:T(8,128)(2,1)S(1)}, bf16[8,128,128]{2,1,0:T(8,128)(2,1)S(1)}, u32[]{:S(2)}, u32[]{:S(2)}) collective-permute-start(bf16[8,128,128]{2,1,0:T(8,128)(2,1)S(1)} %collective-permute-done.7), channel_id=1, source_target_pairs={{0,8},{8,16},{16,24},{1,9},{9,17},{17,25},{2,10},{10,18},{18,26},{... | collective-permute-start | bytes 786440 | tf_op jit(solution)/shard_map/cond/branch_0_fun/ppermute | solution.py:39
  35.0 0.8 %gather_fusion.2 = bf16[32,128,128]{2,1,0:T(8,128)(2,1)S(1)} fusion(bf16[12,128,128]{2,1,0:T(8,128)(2,1)S(1)} %copy.32, s32[1024]{0:T(1024)S(1)} %pad_clamp_fusion.1), kind=kCustom, calls=%fused_computation | custom fusion | bytes 2097280 | tf_op jit(solution)/shard_map/cond/branch_0_fun/gather | solution.py:52
  35.8 1.3 %collective-permute-start.11 = (bf16[8,128,128]{2,1,0:T(8,128)(2,1)S(1)}, bf16[8,128,128]{2,1,0:T(8,128)(2,1)S(1)}, u32[]{:S(2)}, u32[]{:S(2)}) collective-permute-start(bf16[8,128,128]{2,1,0:T(8,128)(2,1)S(1)} %collective-permute-done.10), channel_id=1, source_target_pairs={{8,0},{16,8},{24,16},{9,1},{17,9},{25,17},{10,2},{18,10},{26,18},{... | collective-permute-start | bytes 786440 | tf_op jit(solution)/shard_map/cond/branch_0_fun/ppermute | solution.py:40
  37.1 1.3 %collective-permute-done.8 = bf16[8,128,128]{2,1,0:T(8,128)(2,1)S(1)} collective-permute-done((bf16[8,128,128]{2,1,0:T(8,128)(2,1)S(1)}, bf16[8,128,128]{2,1,0:T(8,128)(2,1)S(1)}, u32[]{:S(2)}, u32[]{:S(2)}) %collective-permute-start.8) | collective-permute-done | bytes 262176 | tf_op jit(solution)/shard_map/cond/branch_0_fun/ppermute | solution.py:39
  38.6 5.4 %collective-permute-done.11 = bf16[8,128,128]{2,1,0:T(8,128)(2,1)S(1)} collective-permute-done((bf16[8,128,128]{2,1,0:T(8,128)(2,1)S(1)}, bf16[8,128,128]{2,1,0:T(8,128)(2,1)S(1)}, u32[]{:S(2)}, u32[]{:S(2)}) %collective-permute-start.11) | collective-permute-done | bytes 262176 | tf_op jit(solution)/shard_map/cond/branch_0_fun/ppermute | solution.py:40
  45.6 1.5 %collective-permute-done.18 = f32[4,128,128]{2,1,0:T(8,128)S(1)} collective-permute-done((f32[4,128,128]{2,1,0:T(8,128)S(1)}, f32[4,128,128]{2,1,0:T(8,128)S(1)}, u32[]{:S(2)}, u32[]{:S(2)}) %collective-permute-start.18) | collective-permute-done | bytes 262176 | tf_op jit(solution)/shard_map/ppermute | solution.py:17
  47.1 1.6 %collective-permute-start.19 = (f32[2,128,128]{2,1,0:T(8,128)S(1)}, f32[2,128,128]{2,1,0:T(8,128)S(1)}, u32[]{:S(2)}, u32[]{:S(2)}) collective-permute-start(f32[2,128,128]{2,1,0:T(8,128)S(1)} %dynamic-slice_bitcast_fusion.1), channel_id=1, source_target_pairs={{0,2},{1,3},{2,0},{3,1},{4,6},{5,7},{6,4},{7,5},{8,10},{9,11},{10,... | collective-permute-start | bytes 393224 | tf_op jit(solution)/shard_map/ppermute | solution.py:17
  48.7 1.4 %iota_reduce_fusion.1 = (pred[8]{0:T(512)(128)(4,1)}, s32[8]{0:T(128)S(1)}) fusion(s32[8]{0:T(128)} %param.10, s32[8]{0:T(128)} %param.12), kind=kLoop, calls=%fused_computation.136 | loop fusion | flops 456 | bytes 104 | tf_op jit(solution)/shard_map/on_device/reduce | solution.py:72
  51.3 1.4 %collective-permute-done.19 = f32[2,128,128]{2,1,0:T(8,128)S(1)} collective-permute-done((f32[2,128,128]{2,1,0:T(8,128)S(1)}, f32[2,128,128]{2,1,0:T(8,128)S(1)}, u32[]{:S(2)}, u32[]{:S(2)}) %collective-permute-start.19) | collective-permute-done | bytes 131104 | tf_op jit(solution)/shard_map/ppermute | solution.py:17
  52.7 1.6 %collective-permute-start.20 = (f32[1,128,128]{2,1,0:T(8,128)S(1)}, f32[1,128,128]{2,1,0:T(8,128)S(1)}, u32[]{:S(2)}, u32[]{:S(2)}) collective-permute-start(f32[1,128,128]{2,1,0:T(8,128)S(1)} %constant_dynamic-slice_fusion.1), channel_id=1, source_target_pairs={{0,4},{1,5},{2,6},{3,7},{4,0},{5,1},{6,2},{7,3},{8,12},{9,13},{10,... | collective-permute-start | bytes 196616 | tf_op jit(solution)/shard_map/ppermute | solution.py:17
  54.4 2.7 %collective-permute-done.20 = f32[1,128,128]{2,1,0:T(8,128)S(1)} collective-permute-done((f32[1,128,128]{2,1,0:T(8,128)S(1)}, f32[1,128,128]{2,1,0:T(8,128)S(1)}, u32[]{:S(2)}, u32[]{:S(2)}) %collective-permute-start.20) | collective-permute-done | bytes 65568 | tf_op jit(solution)/shard_map/ppermute | solution.py:17
  57.1 0.9 %bitcast_select_fusion = bf16[1024,128]{1,0:T(8,128)(2,1)} fusion(pred[1024]{0:T(1024)(128)(4,1)S(1)} %broadcast_bitcast_fusion.1, bf16[128,128]{1,0:T(8,128)(2,1)S(1)} %fusion.40), kind=kLoop, calls=%fused_computation.121 | loop fusion | flops 131072 | bytes 295936 | tf_op jit(solution)/shard_map/jit(_where)/select_n | solution.py:109
  (59 shorter events, 6.2 us)
Async XLA Ops:
  0.0 9.3 %copy-start = (bf16[1536,256]{1,0:T(8,128)(2,1)S(1)}, bf16[1536,256]{1,0:T(8,128)(2,1)}, u32[]{:S(2)}) copy-start(bf16[1536,256]{1,0:T(8,128)(2,1)} %param.9) | copy-start | bytes 2359300
  10.5 10.5 %collective-permute-start.6 = (bf16[8,128,128]{2,1,0:T(8,128)(2,1)S(1)}, bf16[8,128,128]{2,1,0:T(8,128)(2,1)S(1)}, u32[]{:S(2)}, u32[]{:S(2)}) collective-permute-start(bf16[8,128,128]{2,1,0:T(8,128)(2,1)S(1)} %slice_select_fusion), channel_id=1, source_target_pairs={{0,8},{8,16},{16,24},{1,9},{9,17},{17,25},{2,10},{10,18},{18,26},{... | collective-permute-start | bytes 786440 | tf_op jit(solution)/shard_map/cond/branch_0_fun/ppermute | solution.py:39
  15.5 10.0 %collective-permute-start.9 = (bf16[8,128,128]{2,1,0:T(8,128)(2,1)S(1)}, bf16[8,128,128]{2,1,0:T(8,128)(2,1)S(1)}, u32[]{:S(2)}, u32[]{:S(2)}) collective-permute-start(bf16[8,128,128]{2,1,0:T(8,128)(2,1)S(1)} %slice_select_fusion), channel_id=1, source_target_pairs={{8,0},{16,8},{24,16},{9,1},{17,9},{25,17},{10,2},{18,10},{26,18},{... | collective-permute-start | bytes 786440 | tf_op jit(solution)/shard_map/cond/branch_0_fun/ppermute | solution.py:40
  21.0 9.1 %collective-permute-start.7 = (bf16[8,128,128]{2,1,0:T(8,128)(2,1)S(1)}, bf16[8,128,128]{2,1,0:T(8,128)(2,1)S(1)}, u32[]{:S(2)}, u32[]{:S(2)}) collective-permute-start(bf16[8,128,128]{2,1,0:T(8,128)(2,1)S(1)} %collective-permute-done.6), channel_id=1, source_target_pairs={{0,8},{8,16},{16,24},{1,9},{9,17},{17,25},{2,10},{10,18},{18,26},{... | collective-permute-start | bytes 786440 | tf_op jit(solution)/shard_map/cond/branch_0_fun/ppermute | solution.py:39
  25.5 10.3 %collective-permute-start.10 = (bf16[8,128,128]{2,1,0:T(8,128)(2,1)S(1)}, bf16[8,128,128]{2,1,0:T(8,128)(2,1)S(1)}, u32[]{:S(2)}, u32[]{:S(2)}) collective-permute-start(bf16[8,128,128]{2,1,0:T(8,128)(2,1)S(1)} %collective-permute-done.9), channel_id=1, source_target_pairs={{8,0},{16,8},{24,16},{9,1},{17,9},{25,17},{10,2},{18,10},{26,18},{... | collective-permute-start | bytes 786440 | tf_op jit(solution)/shard_map/cond/branch_0_fun/ppermute | solution.py:40
  30.1 8.3 %collective-permute-start.8 = (bf16[8,128,128]{2,1,0:T(8,128)(2,1)S(1)}, bf16[8,128,128]{2,1,0:T(8,128)(2,1)S(1)}, u32[]{:S(2)}, u32[]{:S(2)}) collective-permute-start(bf16[8,128,128]{2,1,0:T(8,128)(2,1)S(1)} %collective-permute-done.7), channel_id=1, source_target_pairs={{0,8},{8,16},{16,24},{1,9},{9,17},{17,25},{2,10},{10,18},{18,26},{... | collective-permute-start | bytes 786440 | tf_op jit(solution)/shard_map/cond/branch_0_fun/ppermute | solution.py:39
  35.8 8.3 %collective-permute-start.11 = (bf16[8,128,128]{2,1,0:T(8,128)(2,1)S(1)}, bf16[8,128,128]{2,1,0:T(8,128)(2,1)S(1)}, u32[]{:S(2)}, u32[]{:S(2)}) collective-permute-start(bf16[8,128,128]{2,1,0:T(8,128)(2,1)S(1)} %collective-permute-done.10), channel_id=1, source_target_pairs={{8,0},{16,8},{24,16},{9,1},{17,9},{25,17},{10,2},{18,10},{26,18},{... | collective-permute-start | bytes 786440 | tf_op jit(solution)/shard_map/cond/branch_0_fun/ppermute | solution.py:40
  45.4 1.6 %collective-permute-start.18 = (f32[4,128,128]{2,1,0:T(8,128)S(1)}, f32[4,128,128]{2,1,0:T(8,128)S(1)}, u32[]{:S(2)}, u32[]{:S(2)}) collective-permute-start(f32[4,128,128]{2,1,0:T(8,128)S(1)} %dynamic-slice_bitcast_fusion), channel_id=1, source_target_pairs={{0,1},{1,0},{2,3},{3,2},{4,5},{5,4},{6,7},{7,6},{8,9},{9,8},{10,11... | collective-permute-start | bytes 786440 | tf_op jit(solution)/shard_map/ppermute | solution.py:17
  47.1 5.6 %collective-permute-start.19 = (f32[2,128,128]{2,1,0:T(8,128)S(1)}, f32[2,128,128]{2,1,0:T(8,128)S(1)}, u32[]{:S(2)}, u32[]{:S(2)}) collective-permute-start(f32[2,128,128]{2,1,0:T(8,128)S(1)} %dynamic-slice_bitcast_fusion.1), channel_id=1, source_target_pairs={{0,2},{1,3},{2,0},{3,1},{4,6},{5,7},{6,4},{7,5},{8,10},{9,11},{10,... | collective-permute-start | bytes 393224 | tf_op jit(solution)/shard_map/ppermute | solution.py:17
  52.7 4.3 %collective-permute-start.20 = (f32[1,128,128]{2,1,0:T(8,128)S(1)}, f32[1,128,128]{2,1,0:T(8,128)S(1)}, u32[]{:S(2)}, u32[]{:S(2)}) collective-permute-start(f32[1,128,128]{2,1,0:T(8,128)S(1)} %constant_dynamic-slice_fusion.1), channel_id=1, source_target_pairs={{0,4},{1,5},{2,6},{3,7},{4,0},{5,1},{6,2},{7,3},{8,12},{9,13},{10,... | collective-permute-start | bytes 196616 | tf_op jit(solution)/shard_map/ppermute | solution.py:17

commit v4 on v3

--- a/solution.py
+++ b/solution.py
@@ -92,7 +92,7 @@
     pick = jnp.repeat(row_for_q[None, :] == jnp.arange(row_tiles)[:, None], tile_edge, axis=1)
     lam_kept = jnp.sum(jnp.where(pick[:, None, :], lam3, jnp.zeros((), lam.dtype)), axis=0)
     lam_kept = lam_kept.reshape(tile_edge, cd_tiles, tile_edge).transpose(1, 0, 2)
-    caps = sorted({max(1, dense // 3), max(1, dense // 2), dense})
+    caps = sorted({max(1, dense // 4), max(1, dense // 3), max(1, dense // 2), dense})
     branch = sum((need > cap).astype(jnp.int32) for cap in caps[:-1])
     partial_sum = lax.switch(
         branch,

time: 58.4 us -> 54.2 us (0.928)
  waiting for transfers between devices: 19.8 us -> 15.2 us
  between operations: 1.54 us -> 2.2 us
    ppermute x3, waiting for transfers between devices: 8.74 us -> 5.4 us  [line_gather(): from_left = lax.ppermute(from_left, axis, rightward)]
    ppermute x3, waiting for transfers between devices: 5.45 us -> 4.24 us  [line_gather(): from_right = lax.ppermute(from_right, axis, leftward)]
where the time goes in v4:
time: 54.2 us; the launch traced here: 53.9 us
  starting transfers between devices  20.8 us (38%)
  waiting for transfers between devices  15.2 us (28%)
  other arithmetic  9.68 us (18%)
  local copies, waits for them, and re-layouts  5.12 us (9%)
  between operations  2.2 us (4%)
    ppermute x3, starting transfers between devices, line_gather(): from_left = lax.ppermute(from_left, axis, rightward)  13.7 us
    ppermute x3, waiting for transfers between devices, halving_reduce_scatter(): parts = keep + lax.ppermute(send, axis, perm)  5.6 us
    ppermute x3, waiting for transfers between devices, line_gather(): from_left = lax.ppermute(from_left, axis, rightward)  5.4 us
    ppermute x3, waiting for transfers between devices, line_gather(): from_right = lax.ppermute(from_right, axis, leftward)  4.24 us
    ppermute x3, starting transfers between devices, line_gather(): from_right = lax.ppermute(from_right, axis, leftward)  3.88 us
    ppermute x3, starting transfers between devices, halving_reduce_scatter(): parts = keep + lax.ppermute(send, axis, perm)  3.21 us
    reduce_sum x1, other arithmetic, on_device(): jnp.sum(jnp.where(pick[:, None, :], lam3, jnp.zeros((), lam.dtype)), axis=0)  2.76 us
    eq x6, local copies, waits for them, and re-layouts, on_device(): kept = cd_sym[:, None] == ab_sym[None, :]  1.72 us
  transfers between devices with their start and end apart: 9, of which 7 were waited for; matrix products, arithmetic and copies ran while one was open for 7% of the time, Pallas kernels for 0%

profile of v4, /device:TPU:0, one launch (start us, length us, event | category | flops | bytes accessed | tf_op | source)
XLA Modules:
  0.0 53.9 jit_solution(10720454546150495476)
XLA Ops:
  0.0 0.7 %eq.201 = s32[4,2]{1,0:T(4,128)S(1)} reshape(s32[8]{0:T(128)} %param.13) | data formatting | bytes 64 | tf_op jit(solution)/shard_map/eq | solution.py:73
  0.8 0.7 %fusion.54 = s32[4]{0:T(128)S(1)} fusion(s32[4,2]{0,1:T(2,128)S(1)} %copy.32, s32[12]{0:T(128)} %param.12), kind=kLoop, calls=%fused_computation.173 | loop fusion | flops 284 | bytes 96 | tf_op jit(solution)/shard_map/reduce_sum | solution.py:75
  1.7 0.7 %eq.204 = s32[12,2]{1,0:T(8,128)S(1)} broadcast(s32[12]{0:T(128)} %param.12), dimensions={0} | broadcast | bytes 144 | tf_op jit(solution)/shard_map/eq | solution.py:73
  5.5 1.3 %iota_reduce_fusion = (pred[12]{0:T(512)(128)(4,1)}, s32[12]{0:T(128)S(1)}) fusion(s32[12]{0:T(128)} %param.12, s32[8]{0:T(128)} %param.11), kind=kLoop, calls=%fused_computation.175 | loop fusion | flops 684 | bytes 140 | tf_op jit(solution)/shard_map/on_device/reduce | solution.py:90
  6.9 2.8 %select_reduce_fusion.4 = bf16[128,1536]{1,0:T(8,128)(2,1)S(1)} fusion(bf16[8,128,1536]{2,1,0:T(8,128)(2,1)} %bitcast.94, pred[8,1536]{1,0:T(8,128)(4,1)S(1)} %broadcast_bitcast_fusion), kind=kLoop, calls=%fused_computation.160 | loop fusion | flops 2949120 | bytes 3551232 | tf_op jit(solution)/shard_map/reduce_sum | solution.py:93
  10.0 31.3 %conditional.1 = (f32[4,2,128,128]{3,2,1,0:T(8,128)S(1)}) conditional(s32[]{:T(128)} %clamp.3, (s32[4,1]{0,1:T(1,128)S(1)}, s32[4,24]{1,0:T(4,128)S(1)}, s32[4,24]{1,0:T(4,128)S(1)}, pred[4,24,24]{2,1,0:T(8,128)(4,1)S(1)}, s32[4,24]{1,0:T(4,128)S(1)}, /*index=5*/s32[4,24]{1,0:T(4,128)S(1)}, s32[4,24]{1,0:T(4,128)S(1)}, ...), branch_computations={%region_7.10_spmd, %region_10.13_spmd, %region_13.16_spmd, %region... | conditional | flops 411180288 | bytes 81549152 | solution.py:97
  11.4 4.9 %collective-permute-start.6 = (bf16[6,128,128]{2,1,0:T(8,128)(2,1)S(1)}, bf16[6,128,128]{2,1,0:T(8,128)(2,1)S(1)}, u32[]{:S(2)}, u32[]{:S(2)}) collective-permute-start(bf16[6,128,128]{2,1,0:T(8,128)(2,1)S(1)} %slice_select_fusion), channel_id=1, source_target_pairs={{0,8},{8,16},{16,24},{1,9},{9,17},{17,25},{2,10},{10,18},{18,26},{... | collective-permute-start | bytes 589832 | tf_op jit(solution)/shard_map/cond/branch_0_fun/ppermute | solution.py:39
  16.4 1.3 %collective-permute-start.9 = (bf16[6,128,128]{2,1,0:T(8,128)(2,1)S(1)}, bf16[6,128,128]{2,1,0:T(8,128)(2,1)S(1)}, u32[]{:S(2)}, u32[]{:S(2)}) collective-permute-start(bf16[6,128,128]{2,1,0:T(8,128)(2,1)S(1)} %slice_select_fusion), channel_id=1, source_target_pairs={{8,0},{16,8},{24,16},{9,1},{17,9},{25,17},{10,2},{18,10},{26,18},{... | collective-permute-start | bytes 589832 | tf_op jit(solution)/shard_map/cond/branch_0_fun/ppermute | solution.py:40
  18.2 0.7 %gather_fusion.2 = bf16[24,128,128]{2,1,0:T(8,128)(2,1)S(1)} fusion(bf16[12,128,128]{2,1,0:T(8,128)(2,1)S(1)} %copy.35, s32[1024]{0:T(1024)S(1)} %pad_clamp_fusion.1), kind=kCustom, calls=%fused_computation | custom fusion | bytes 1572960 | tf_op jit(solution)/shard_map/cond/branch_0_fun/gather | solution.py:52
  18.9 1.6 %collective-permute-done.6 = bf16[6,128,128]{2,1,0:T(8,128)(2,1)S(1)} collective-permute-done((bf16[6,128,128]{2,1,0:T(8,128)(2,1)S(1)}, bf16[6,128,128]{2,1,0:T(8,128)(2,1)S(1)}, u32[]{:S(2)}, u32[]{:S(2)}) %collective-permute-start.6) | collective-permute-done | bytes 196640 | tf_op jit(solution)/shard_map/cond/branch_0_fun/ppermute | solution.py:39
  20.5 4.4 %collective-permute-start.7 = (bf16[6,128,128]{2,1,0:T(8,128)(2,1)S(1)}, bf16[6,128,128]{2,1,0:T(8,128)(2,1)S(1)}, u32[]{:S(2)}, u32[]{:S(2)}) collective-permute-start(bf16[6,128,128]{2,1,0:T(8,128)(2,1)S(1)} %collective-permute-done.6), channel_id=1, source_target_pairs={{0,8},{8,16},{16,24},{1,9},{9,17},{17,25},{2,10},{10,18},{18,26},{... | collective-permute-start | bytes 589832 | tf_op jit(solution)/shard_map/cond/branch_0_fun/ppermute | solution.py:39
  24.9 1.3 %collective-permute-start.10 = (bf16[6,128,128]{2,1,0:T(8,128)(2,1)S(1)}, bf16[6,128,128]{2,1,0:T(8,128)(2,1)S(1)}, u32[]{:S(2)}, u32[]{:S(2)}) collective-permute-start(bf16[6,128,128]{2,1,0:T(8,128)(2,1)S(1)} %collective-permute-done.9), channel_id=1, source_target_pairs={{8,0},{16,8},{24,16},{9,1},{17,9},{25,17},{10,2},{18,10},{26,18},{... | collective-permute-start | bytes 589832 | tf_op jit(solution)/shard_map/cond/branch_0_fun/ppermute | solution.py:40
  26.2 1.9 %collective-permute-done.7 = bf16[6,128,128]{2,1,0:T(8,128)(2,1)S(1)} collective-permute-done((bf16[6,128,128]{2,1,0:T(8,128)(2,1)S(1)}, bf16[6,128,128]{2,1,0:T(8,128)(2,1)S(1)}, u32[]{:S(2)}, u32[]{:S(2)}) %collective-permute-start.7) | collective-permute-done | bytes 196640 | tf_op jit(solution)/shard_map/cond/branch_0_fun/ppermute | solution.py:39
  28.2 4.4 %collective-permute-start.8 = (bf16[6,128,128]{2,1,0:T(8,128)(2,1)S(1)}, bf16[6,128,128]{2,1,0:T(8,128)(2,1)S(1)}, u32[]{:S(2)}, u32[]{:S(2)}) collective-permute-start(bf16[6,128,128]{2,1,0:T(8,128)(2,1)S(1)} %collective-permute-done.7), channel_id=1, source_target_pairs={{0,8},{8,16},{16,24},{1,9},{9,17},{17,25},{2,10},{10,18},{18,26},{... | collective-permute-start | bytes 589832 | tf_op jit(solution)/shard_map/cond/branch_0_fun/ppermute | solution.py:39
  32.6 1.3 %collective-permute-start.11 = (bf16[6,128,128]{2,1,0:T(8,128)(2,1)S(1)}, bf16[6,128,128]{2,1,0:T(8,128)(2,1)S(1)}, u32[]{:S(2)}, u32[]{:S(2)}) collective-permute-start(bf16[6,128,128]{2,1,0:T(8,128)(2,1)S(1)} %collective-permute-done.10), channel_id=1, source_target_pairs={{8,0},{16,8},{24,16},{9,1},{17,9},{25,17},{10,2},{18,10},{26,18},{... | collective-permute-start | bytes 589832 | tf_op jit(solution)/shard_map/cond/branch_0_fun/ppermute | solution.py:40
  33.9 1.8 %collective-permute-done.8 = bf16[6,128,128]{2,1,0:T(8,128)(2,1)S(1)} collective-permute-done((bf16[6,128,128]{2,1,0:T(8,128)(2,1)S(1)}, bf16[6,128,128]{2,1,0:T(8,128)(2,1)S(1)}, u32[]{:S(2)}, u32[]{:S(2)}) %collective-permute-start.8) | collective-permute-done | bytes 196640 | tf_op jit(solution)/shard_map/cond/branch_0_fun/ppermute | solution.py:39
  35.9 4.2 %collective-permute-done.11 = bf16[6,128,128]{2,1,0:T(8,128)(2,1)S(1)} collective-permute-done((bf16[6,128,128]{2,1,0:T(8,128)(2,1)S(1)}, bf16[6,128,128]{2,1,0:T(8,128)(2,1)S(1)}, u32[]{:S(2)}, u32[]{:S(2)}) %collective-permute-start.11) | collective-permute-done | bytes 196640 | tf_op jit(solution)/shard_map/cond/branch_0_fun/ppermute | solution.py:40
  41.5 1.5 %collective-permute-done.24 = f32[4,128,128]{2,1,0:T(8,128)S(1)} collective-permute-done((f32[4,128,128]{2,1,0:T(8,128)S(1)}, f32[4,128,128]{2,1,0:T(8,128)S(1)}, u32[]{:S(2)}, u32[]{:S(2)}) %collective-permute-start.24) | collective-permute-done | bytes 262176 | tf_op jit(solution)/shard_map/ppermute | solution.py:17
  43.0 1.6 %collective-permute-start.25 = (f32[2,128,128]{2,1,0:T(8,128)S(1)}, f32[2,128,128]{2,1,0:T(8,128)S(1)}, u32[]{:S(2)}, u32[]{:S(2)}) collective-permute-start(f32[2,128,128]{2,1,0:T(8,128)S(1)} %dynamic-slice_bitcast_fusion.1), channel_id=1, source_target_pairs={{0,2},{1,3},{2,0},{3,1},{4,6},{5,7},{6,4},{7,5},{8,10},{9,11},{10,... | collective-permute-start | bytes 393224 | tf_op jit(solution)/shard_map/ppermute | solution.py:17
  44.6 1.4 %iota_reduce_fusion.1 = (pred[8]{0:T(512)(128)(4,1)}, s32[8]{0:T(128)S(1)}) fusion(s32[8]{0:T(128)} %param.11, s32[8]{0:T(128)} %param.13), kind=kLoop, calls=%fused_computation.176 | loop fusion | flops 456 | bytes 104 | tf_op jit(solution)/shard_map/on_device/reduce | solution.py:72
  47.2 1.4 %collective-permute-done.25 = f32[2,128,128]{2,1,0:T(8,128)S(1)} collective-permute-done((f32[2,128,128]{2,1,0:T(8,128)S(1)}, f32[2,128,128]{2,1,0:T(8,128)S(1)}, u32[]{:S(2)}, u32[]{:S(2)}) %collective-permute-start.25) | collective-permute-done | bytes 131104 | tf_op jit(solution)/shard_map/ppermute | solution.py:17
  48.6 1.6 %collective-permute-start.26 = (f32[1,128,128]{2,1,0:T(8,128)S(1)}, f32[1,128,128]{2,1,0:T(8,128)S(1)}, u32[]{:S(2)}, u32[]{:S(2)}) collective-permute-start(f32[1,128,128]{2,1,0:T(8,128)S(1)} %constant_dynamic-slice_fusion.1), channel_id=1, source_target_pairs={{0,4},{1,5},{2,6},{3,7},{4,0},{5,1},{6,2},{7,3},{8,12},{9,13},{10,... | collective-permute-start | bytes 196616 | tf_op jit(solution)/shard_map/ppermute | solution.py:17
  50.3 2.7 %collective-permute-done.26 = f32[1,128,128]{2,1,0:T(8,128)S(1)} collective-permute-done((f32[1,128,128]{2,1,0:T(8,128)S(1)}, f32[1,128,128]{2,1,0:T(8,128)S(1)}, u32[]{:S(2)}, u32[]{:S(2)}) %collective-permute-start.26) | collective-permute-done | bytes 65568 | tf_op jit(solution)/shard_map/ppermute | solution.py:17
  53.0 0.9 %bitcast_select_fusion = bf16[1024,128]{1,0:T(8,128)(2,1)} fusion(pred[1024]{0:T(1024)(128)(4,1)S(1)} %broadcast_bitcast_fusion.1, bf16[128,128]{1,0:T(8,128)(2,1)S(1)} %fusion.53), kind=kLoop, calls=%fused_computation.161 | loop fusion | flops 131072 | bytes 295936 | tf_op jit(solution)/shard_map/jit(_where)/select_n | solution.py:109
  (58 shorter events, 6.1 us)
Async XLA Ops:
  6.9 3.1 %copy-start = (bf16[1536,256]{1,0:T(8,128)(2,1)S(1)}, bf16[1536,256]{1,0:T(8,128)(2,1)}, u32[]{:S(2)}) copy-start(bf16[1536,256]{1,0:T(8,128)(2,1)} %param.10) | copy-start | bytes 2359300
  11.4 9.1 %collective-permute-start.6 = (bf16[6,128,128]{2,1,0:T(8,128)(2,1)S(1)}, bf16[6,128,128]{2,1,0:T(8,128)(2,1)S(1)}, u32[]{:S(2)}, u32[]{:S(2)}) collective-permute-start(bf16[6,128,128]{2,1,0:T(8,128)(2,1)S(1)} %slice_select_fusion), channel_id=1, source_target_pairs={{0,8},{8,16},{16,24},{1,9},{9,17},{17,25},{2,10},{10,18},{18,26},{... | collective-permute-start | bytes 589832 | tf_op jit(solution)/shard_map/cond/branch_0_fun/ppermute | solution.py:39
  16.4 8.5 %collective-permute-start.9 = (bf16[6,128,128]{2,1,0:T(8,128)(2,1)S(1)}, bf16[6,128,128]{2,1,0:T(8,128)(2,1)S(1)}, u32[]{:S(2)}, u32[]{:S(2)}) collective-permute-start(bf16[6,128,128]{2,1,0:T(8,128)(2,1)S(1)} %slice_select_fusion), channel_id=1, source_target_pairs={{8,0},{16,8},{24,16},{9,1},{17,9},{25,17},{10,2},{18,10},{26,18},{... | collective-permute-start | bytes 589832 | tf_op jit(solution)/shard_map/cond/branch_0_fun/ppermute | solution.py:40
  20.5 7.7 %collective-permute-start.7 = (bf16[6,128,128]{2,1,0:T(8,128)(2,1)S(1)}, bf16[6,128,128]{2,1,0:T(8,128)(2,1)S(1)}, u32[]{:S(2)}, u32[]{:S(2)}) collective-permute-start(bf16[6,128,128]{2,1,0:T(8,128)(2,1)S(1)} %collective-permute-done.6), channel_id=1, source_target_pairs={{0,8},{8,16},{16,24},{1,9},{9,17},{17,25},{2,10},{10,18},{18,26},{... | collective-permute-start | bytes 589832 | tf_op jit(solution)/shard_map/cond/branch_0_fun/ppermute | solution.py:39
  24.9 7.6 %collective-permute-start.10 = (bf16[6,128,128]{2,1,0:T(8,128)(2,1)S(1)}, bf16[6,128,128]{2,1,0:T(8,128)(2,1)S(1)}, u32[]{:S(2)}, u32[]{:S(2)}) collective-permute-start(bf16[6,128,128]{2,1,0:T(8,128)(2,1)S(1)} %collective-permute-done.9), channel_id=1, source_target_pairs={{8,0},{16,8},{24,16},{9,1},{17,9},{25,17},{10,2},{18,10},{26,18},{... | collective-permute-start | bytes 589832 | tf_op jit(solution)/shard_map/cond/branch_0_fun/ppermute | solution.py:40
  28.2 7.6 %collective-permute-start.8 = (bf16[6,128,128]{2,1,0:T(8,128)(2,1)S(1)}, bf16[6,128,128]{2,1,0:T(8,128)(2,1)S(1)}, u32[]{:S(2)}, u32[]{:S(2)}) collective-permute-start(bf16[6,128,128]{2,1,0:T(8,128)(2,1)S(1)} %collective-permute-done.7), channel_id=1, source_target_pairs={{0,8},{8,16},{16,24},{1,9},{9,17},{17,25},{2,10},{10,18},{18,26},{... | collective-permute-start | bytes 589832 | tf_op jit(solution)/shard_map/cond/branch_0_fun/ppermute | solution.py:39
  32.6 7.6 %collective-permute-start.11 = (bf16[6,128,128]{2,1,0:T(8,128)(2,1)S(1)}, bf16[6,128,128]{2,1,0:T(8,128)(2,1)S(1)}, u32[]{:S(2)}, u32[]{:S(2)}) collective-permute-start(bf16[6,128,128]{2,1,0:T(8,128)(2,1)S(1)} %collective-permute-done.10), channel_id=1, source_target_pairs={{8,0},{16,8},{24,16},{9,1},{17,9},{25,17},{10,2},{18,10},{26,18},{... | collective-permute-start | bytes 589832 | tf_op jit(solution)/shard_map/cond/branch_0_fun/ppermute | solution.py:40
  41.3 1.6 %collective-permute-start.24 = (f32[4,128,128]{2,1,0:T(8,128)S(1)}, f32[4,128,128]{2,1,0:T(8,128)S(1)}, u32[]{:S(2)}, u32[]{:S(2)}) collective-permute-start(f32[4,128,128]{2,1,0:T(8,128)S(1)} %dynamic-slice_bitcast_fusion), channel_id=1, source_target_pairs={{0,1},{1,0},{2,3},{3,2},{4,5},{5,4},{6,7},{7,6},{8,9},{9,8},{10,11... | collective-permute-start | bytes 786440 | tf_op jit(solution)/shard_map/ppermute | solution.py:17
  43.0 5.6 %collective-permute-start.25 = (f32[2,128,128]{2,1,0:T(8,128)S(1)}, f32[2,128,128]{2,1,0:T(8,128)S(1)}, u32[]{:S(2)}, u32[]{:S(2)}) collective-permute-start(f32[2,128,128]{2,1,0:T(8,128)S(1)} %dynamic-slice_bitcast_fusion.1), channel_id=1, source_target_pairs={{0,2},{1,3},{2,0},{3,1},{4,6},{5,7},{6,4},{7,5},{8,10},{9,11},{10,... | collective-permute-start | bytes 393224 | tf_op jit(solution)/shard_map/ppermute | solution.py:17
  48.6 4.3 %collective-permute-start.26 = (f32[1,128,128]{2,1,0:T(8,128)S(1)}, f32[1,128,128]{2,1,0:T(8,128)S(1)}, u32[]{:S(2)}, u32[]{:S(2)}) collective-permute-start(f32[1,128,128]{2,1,0:T(8,128)S(1)} %constant_dynamic-slice_fusion.1), channel_id=1, source_target_pairs={{0,4},{1,5},{2,6},{3,7},{4,0},{5,1},{6,2},{7,3},{8,12},{9,13},{10,... | collective-permute-start | bytes 196616 | tf_op jit(solution)/shard_map/ppermute | solution.py:17
